TPU v7x, 32 devices: a whole 2x2x4 slice. The times are simulated.
32 devices in a mesh: ctx: 4 (over z), row: 8 (over y, x, core).
Axes of the slice: x: 2, y: 2, z: 4, core: 2. Of those that a mesh axis runs over, the one named last changes fastest.
Arguments:
- queries: bfloat16 [2048, 2048], P('row'), may hold values from -120 to 120
- keys: bfloat16 [1536, 2048], P('ctx'), may hold values from -5 to 5
- values: bfloat16 [1536, 2048], P('ctx'), may hold values from -6 to 6
- block_list: int32 [16, 8], P('row'), may hold values from 0 to 11, as said below
- block_count: int32 [16], P('row'), may hold values from 1 to 8, as said below
Outputs:
- owned: bfloat16 [2048, 2048], P('row', 'ctx')
Inputs may be any that keep to these rules, and one draw needn't show every extreme that they name: `block_list`: entries of one list are distinct; the first entry of the list of query block b is b % 12. Entries past block_count are ignored. `block_count`: every query block uses at least one list entry.
All inputs are finite; a program needn't handle non-finite values.
Results may differ from a plain program's by a relative error of at most 0.0044.
Values may be sent and summed in bfloat16 or wider, within the bound.
No kernel may reach another device: no remote copies, remote signals or barrier semaphores. Data moves between devices by JAX's collectives and lax.ppermute only.
A program may use at most 64 MiB of HBM per device.

v0:
```python
import jax
import jax.numpy as jnp
from jax import lax
from jax.sharding import PartitionSpec as P

HEADS = 16
HEAD_DIM = 128
BLOCK = 128


masked_fill = -1e30


def combine_rows(pieces):
    maxima, totals, partial_out = pieces
    item_rows, sources, head_share = maxima.shape
    row_best = jnp.max(maxima, axis=1)
    weight = jnp.exp(maxima - row_best[:, None, :])
    total_sum = jnp.sum(totals * weight, axis=1)
    out_heads = partial_out.reshape(item_rows, sources, head_share, HEAD_DIM)
    numerator = jnp.sum(out_heads * weight[:, :, :, None], axis=1)
    return (numerator / total_sum[:, :, None]).reshape(item_rows, head_share * HEAD_DIM)


def chosen_range(block_list, block_count, first_block, block_span):
    slot_live = jnp.arange(block_list.shape[1], dtype=jnp.int32)[None, :] < block_count[:, None]
    block_ids = first_block + jnp.arange(block_span, dtype=jnp.int32)
    block_hits = (block_list[:, :, None] == block_ids[None, None, :]) & slot_live[:, :, None]
    return jnp.any(block_hits, axis=1)


def segment_parts(query_heads, key_heads, value_heads, chosen):
    key_live = jnp.repeat(jnp.repeat(chosen, BLOCK, axis=0), BLOCK, axis=1)[None, :, :]
    score_scale = 1.0 / HEAD_DIM**0.5
    scores = (
        jnp.einsum("qhd,khd->hqk", query_heads, key_heads, preferred_element_type=jnp.float32)
        * score_scale
    )
    seg_max = jnp.max(jnp.where(key_live, scores, masked_fill), axis=2)
    probs_live = jnp.where(key_live, jnp.exp(scores - seg_max[:, :, None]), 0.0)
    seg_total = jnp.sum(probs_live, axis=2)
    probs_low = probs_live.astype(jnp.bfloat16)
    seg_out = jnp.einsum("hqk,khd->qhd", probs_low, value_heads, preferred_element_type=jnp.float32)
    return (seg_max, seg_total, seg_out)


def local_parts(queries, keys, values, block_list, block_count):
    row_count = queries.shape[0]
    ctx_span = keys.shape[0]
    blocks_here = ctx_span // BLOCK
    chosen = chosen_range(block_list, block_count, lax.axis_index("ctx") * blocks_here, blocks_here)
    return segment_parts(
        queries.reshape(row_count, HEADS, HEAD_DIM),
        keys.reshape(ctx_span, HEADS, HEAD_DIM),
        values.reshape(ctx_span, HEADS, HEAD_DIM),
        chosen,
    )


def local(queries, keys, values, block_list, block_count):
    row_count = queries.shape[0]
    shards = lax.axis_size("ctx")
    head_share = HEADS // shards
    share_width = head_share * HEAD_DIM
    seg_max, seg_total, seg_out = local_parts(queries, keys, values, block_list, block_count)
    sent = (
        jnp.transpose(seg_max)[:, None, :],
        jnp.transpose(seg_total)[:, None, :],
        seg_out.reshape(row_count, 1, HEADS * HEAD_DIM),
    )
    attended = combine_rows(
        (
            lax.all_to_all(sent[0], "ctx", split_axis=2, concat_axis=1, tiled=True),
            lax.all_to_all(sent[1], "ctx", split_axis=2, concat_axis=1, tiled=True),
            lax.all_to_all(sent[2], "ctx", split_axis=2, concat_axis=1, tiled=True),
        )
    )
    attended_low = attended.astype(jnp.bfloat16)
    owners = lax.axis_size("row")
    per_owner = row_count // owners
    grouped = attended_low.reshape(per_owner, owners, share_width)
    regrouped = lax.all_to_all(grouped, "row", split_axis=1, concat_axis=0, tiled=True)
    return regrouped.reshape(row_count, share_width)


def solution(mesh):
    return jax.shard_map(
        local,
        mesh=mesh,
        in_specs=(P("row", None), P("ctx", None), P("ctx", None), P("row", None), P("row")),
        out_specs=P("row", "ctx"),
        check_vma=False,
    )
```

profile of v0, /device:TPU:0, one launch (start us, length us, event | category | flops | bytes accessed | tf_op | source)
XLA Modules:
  0.0 105.7 jit_solution(18359404160349722766)
XLA Ops:
  0.0 0.0 copy-start
  0.0 0.8 iota_compare_fusion
  0.9 0.9 and_reduce_fusion
  1.7 0.1 broadcast_bitcast_fusion
  1.8 0.2 copy.27
  2.0 0.0 copy-done
  2.0 5.2 %select_reduce_fusion = (f32[16,256]{1,0:T(8,128)S(1)}, f32[16,256,384]{2,1,0:T(8,128)}) fusion(pred[256,384]{1,0:T(8,128)(4,1)S(1)} %copy.27, bf16[384,2048]{1,0:T(8,128)(2,1)S(1)} %copy-done, bf16[256,2048]{1,0:T(8,128)(2,1)} %param.5), kind=kOutput, calls=%fused_computation.1 | convolution fusion | flops 407367680 | bytes 9027584 | tf_op jit(solution)/shard_map/qhd,khd->hqk/dot_general | solution.py:36
  7.2 0.6 broadcast_in_dim.47
  7.9 6.3 %all-to-all-start.1 = ((f32[256,1,16]{0,1,2:T(1,128)}), f32[256,1,16]{0,1,2:T(1,128)S(1)}, u32[]{:S(2)}, u32[]{:S(2)}) async-start(f32[256,1,16]{0,1,2:T(1,128)} %broadcast_in_dim.47), calls=%async_computation.1 | async-start | bytes 32768 | tf_op jit(solution)/shard_map/all_to_all | solution.py:73
  14.2 0.0 copy-start.1
  14.2 4.0 %fusion = f32[16,256]{1,0:T(8,128)S(1)} fusion(f32[16,256,384]{2,1,0:T(8,128)} %get-tuple-element.8, f32[16,256]{1,0:T(8,128)S(1)} %get-tuple-element.7, pred[256,384]{1,0:T(8,128)(4,1)S(1)} %copy.27), kind=kLoop, calls=%fused_computation.2 | loop fusion | flops 6287360 | bytes 6422528 | tf_op jit(solution)/shard_map/reduce_sum | solution.py:41
  18.1 0.0 copy-done.1
  18.2 1.6 %copy.36 = bf16[384,2048]{0,1:T(8,128)(2,1)} copy(bf16[384,2048]{1,0:T(8,128)(2,1)S(1)} %copy-done.1) | data formatting | bytes 3145728 | tf_op jit(solution)/shard_map/reshape | solution.py:55
  19.7 0.6 broadcast_in_dim.48
  20.3 0.0 all-to-all-done.1
  20.3 5.1 %all-to-all-start.2 = ((f32[256,1,16]{0,1,2:T(1,128)}), f32[256,1,16]{0,1,2:T(1,128)S(1)}, u32[]{:S(2)}, u32[]{:S(2)}) async-start(f32[256,1,16]{0,1,2:T(1,128)} %broadcast_in_dim.48), calls=%async_computation.2 | async-start | bytes 32768 | tf_op jit(solution)/shard_map/all_to_all | solution.py:74
  25.4 4.2 %fusion.2 = f32[16,256,128]{1,2,0:T(8,128)S(1)} fusion(bf16[384,16,128]{0,2,1:T(8,128)(2,1)} %bitcast.49, f32[16,256,384]{2,1,0:T(8,128)} %get-tuple-element.8, f32[16,256]{1,0:T(8,128)S(1)} %get-tuple-element.7, pred[256,384]{1,0:T(8,128)(4,1)S(1)} %copy.27), kind=kOutput, calls=%fused_computation.4 | convolution fusion | flops 408944640 | bytes 10076160 | tf_op jit(solution)/shard_map/hqk,khd->qhd/dot_general | solution.py:43
  29.6 10.0 %copy.31 = f32[256,1,2048]{0,1,2:T(1,128)} copy(f32[256,1,2048]{0,2,1:T(8,128)S(1)} %bitcast.48) | data formatting | bytes 4194304 | tf_op jit(solution)/shard_map/reshape | solution.py:69
  39.6 0.0 all-to-all-done.2
  39.6 5.1 %all-to-all-start = ((f32[256,1,2048]{0,1,2:T(1,128)}), f32[256,1,2048]{0,1,2:T(1,128)}, u32[]{:S(2)}, u32[]{:S(2)}) async-start(f32[256,1,2048]{0,1,2:T(1,128)} %copy.31), calls=%async_computation | async-start | bytes 4194304 | tf_op jit(solution)/shard_map/all_to_all | solution.py:75
  44.9 0.1 copy.34
  45.0 0.3 div.12
  45.4 0.2 div.13
  45.6 46.3 %all-to-all-done = f32[256,1,2048]{0,1,2:T(1,128)} async-done(((f32[256,1,2048]{0,1,2:T(1,128)}), f32[256,1,2048]{0,1,2:T(1,128)}, u32[]{:S(2)}, u32[]{:S(2)}) %all-to-all-start) | async-done | bytes 2097184 | tf_op jit(solution)/shard_map/all_to_all | solution.py:75
  91.9 0.2 mul.38
  92.1 2.0 %fusion.8 = f32[256,512]{0,1:T(8,128)S(1)} fusion(f32[256,1,4,512]{0,3,2,1:T(8,128)S(1)} %bitcast.47, f32[256,1,4,512]{0,1,3,2:T(1,128)} %bitcast.5), kind=kLoop, calls=%fused_computation.10 | loop fusion | flops 917504 | bytes 4718592 | tf_op jit(solution)/shard_map/reduce_sum | solution.py:21
  94.1 0.2 copy.33
  94.3 0.1 fusion.14
  94.4 0.1 copy.35
  94.5 10.5 %all_to_all.51 = bf16[32,8,512]{2,0,1:T(8,128)(2,1)S(1)} all-to-all(bf16[32,8,512]{2,0,1:T(8,128)(2,1)S(1)} %copy.35), channel_id=1, replica_groups=mesh['ctx'=4,'row'=8] {'row'}, dimensions={1} | all-to-all | bytes 524288 | tf_op jit(solution)/shard_map/all_to_all | solution.py:82
  105.0 0.7 copy.57
  (8 shorter events, 0.2 us)
Async XLA Ops:
  0.0 2.0 %copy-start = (bf16[384,2048]{1,0:T(8,128)(2,1)S(1)}, bf16[384,2048]{1,0:T(8,128)(2,1)}, u32[]{:S(2)}) copy-start(bf16[384,2048]{1,0:T(8,128)(2,1)} %param.6) | copy-start | bytes 4718596
  7.9 12.5 %all-to-all-start.1 = ((f32[256,1,16]{0,1,2:T(1,128)}), f32[256,1,16]{0,1,2:T(1,128)S(1)}, u32[]{:S(2)}, u32[]{:S(2)}) async-start(f32[256,1,16]{0,1,2:T(1,128)} %broadcast_in_dim.47), calls=%async_computation.1 | async-start | bytes 32768 | tf_op jit(solution)/shard_map/all_to_all | solution.py:73
  14.2 4.0 %copy-start.1 = (bf16[384,2048]{1,0:T(8,128)(2,1)S(1)}, bf16[384,2048]{1,0:T(8,128)(2,1)}, u32[]{:S(2)}) copy-start(bf16[384,2048]{1,0:T(8,128)(2,1)} %param.7) | copy-start | bytes 4718596
  20.3 19.3 %all-to-all-start.2 = ((f32[256,1,16]{0,1,2:T(1,128)}), f32[256,1,16]{0,1,2:T(1,128)S(1)}, u32[]{:S(2)}, u32[]{:S(2)}) async-start(f32[256,1,16]{0,1,2:T(1,128)} %broadcast_in_dim.48), calls=%async_computation.2 | async-start | bytes 32768 | tf_op jit(solution)/shard_map/all_to_all | solution.py:74
  39.6 52.3 %all-to-all-start = ((f32[256,1,2048]{0,1,2:T(1,128)}), f32[256,1,2048]{0,1,2:T(1,128)}, u32[]{:S(2)}, u32[]{:S(2)}) async-start(f32[256,1,2048]{0,1,2:T(1,128)} %copy.31), calls=%async_computation | async-start | bytes 4194304 | tf_op jit(solution)/shard_map/all_to_all | solution.py:75
where the time goes:
time: 106 us
  waiting for transfers between devices  46.3 us (44%)
  starting transfers between devices  16.5 us (16%)
  local copies, waits for them, and re-layouts  15 us (14%)
  blocking collectives  10.5 us (10%)
  matrix products  9.4 us (9%)
  other arithmetic  7.93 us (7%)
    all_to_all x1, waiting for transfers between devices, local(): lax.all_to_all(sent[2], 'ctx', split_axis=2, concat_axis=1, tiled=True)  46.3 us
    all_to_all x1, blocking collectives, local(): lax.all_to_all(grouped, 'row', split_axis=1, concat_axis=0, tiled=True)  10.5 us
    reshape x1, local copies, waits for them, and re-layouts, local(): seg_out.reshape(row_count, 1, HEADS * HEAD_DIM)  10 us
    all_to_all x1, starting transfers between devices, local(): lax.all_to_all(sent[0], 'ctx', split_axis=2, concat_axis=1, tiled=True)  6.32 us
    dot_general x1, matrix products, segment_parts(): jnp.einsum('qhd,khd->hqk', query_heads, key_heads, preferred_element_type...  5.2 us
    all_to_all x1, starting transfers between devices, local(): lax.all_to_all(sent[2], 'ctx', split_axis=2, concat_axis=1, tiled=True)  5.09 us
    all_to_all x1, starting transfers between devices, local(): lax.all_to_all(sent[1], 'ctx', split_axis=2, concat_axis=1, tiled=True)  5.09 us
    dot_general x1, matrix products, segment_parts(): jnp.einsum('hqk,khd->qhd', probs_low, value_heads, preferred_element_type...  4.2 us
  transfers between devices with their start and end apart: 3, of which 1 were waited for; matrix products, arithmetic and copies ran while one was open for 20% of the time, Pallas kernels for 0%

commit v1 on v0

v1 whole, which is shorter than its diff:
```python
import jax
import jax.numpy as jnp
from jax import lax
from jax.sharding import PartitionSpec as P

HEADS = 16
HEAD_DIM = 128
BLOCK = 128


masked_fill = -1e30


def chosen_range(block_list, block_count, first_block, block_span):
    slot_live = jnp.arange(block_list.shape[1], dtype=jnp.int32)[None, :] < block_count[:, None]
    block_ids = first_block + jnp.arange(block_span, dtype=jnp.int32)
    block_hits = (block_list[:, :, None] == block_ids[None, None, :]) & slot_live[:, :, None]
    return jnp.any(block_hits, axis=1)


def segment_parts(query_heads, key_heads, value_heads, chosen):
    key_live = jnp.repeat(jnp.repeat(chosen, BLOCK, axis=0), BLOCK, axis=1)[None, :, :]
    score_scale = 1.0 / HEAD_DIM**0.5
    scores = (
        jnp.einsum("qhd,khd->hqk", query_heads, key_heads, preferred_element_type=jnp.float32)
        * score_scale
    )
    seg_max = jnp.max(jnp.where(key_live, scores, masked_fill), axis=2)
    probs_live = jnp.where(key_live, jnp.exp(scores - seg_max[:, :, None]), 0.0)
    seg_total = jnp.sum(probs_live, axis=2)
    probs_low = probs_live.astype(jnp.bfloat16)
    seg_out = jnp.einsum("hqk,khd->hqd", probs_low, value_heads, preferred_element_type=jnp.float32)
    return (seg_max, seg_total, seg_out)


def local(queries, keys, values, block_list, block_count):
    row_count = queries.shape[0]
    ctx_span = keys.shape[0]
    shards = lax.axis_size("ctx")
    head_share = HEADS // shards
    share_width = head_share * HEAD_DIM
    blocks_here = ctx_span // BLOCK
    chosen = chosen_range(block_list, block_count, lax.axis_index("ctx") * blocks_here, blocks_here)
    seg_max, seg_total, seg_out = segment_parts(
        queries.reshape(row_count, HEADS, HEAD_DIM),
        keys.reshape(ctx_span, HEADS, HEAD_DIM),
        values.reshape(ctx_span, HEADS, HEAD_DIM),
        chosen,
    )
    stats = jnp.stack(
        [seg_max.reshape(shards, head_share, row_count), seg_total.reshape(shards, head_share, row_count)],
        axis=1,
    )
    part_low = seg_out.astype(jnp.bfloat16).reshape(shards, head_share, row_count, HEAD_DIM)
    stats_in = lax.all_to_all(stats, "ctx", 0, 0, tiled=True)
    part_in = lax.all_to_all(part_low, "ctx", 0, 0, tiled=True)
    maxima = stats_in[:, 0]
    totals = stats_in[:, 1]
    row_best = jnp.max(maxima, axis=0)
    weight = jnp.exp(maxima - row_best[None])
    total_sum = jnp.sum(totals * weight, axis=0)
    numerator = jnp.sum(part_in.astype(jnp.float32) * weight[:, :, :, None], axis=0)
    attended = numerator / total_sum[:, :, None]
    attended_low = jnp.transpose(attended, (1, 0, 2)).reshape(row_count, share_width).astype(jnp.bfloat16)
    owners = lax.axis_size("row")
    per_owner = row_count // owners
    grouped = jnp.transpose(attended_low.reshape(per_owner, owners, share_width), (1, 0, 2))
    regrouped = lax.all_to_all(grouped, "row", 0, 0, tiled=True)
    return regrouped.reshape(row_count, share_width)


def solution(mesh):
    return jax.shard_map(
        local,
        mesh=mesh,
        in_specs=(P("row", None), P("ctx", None), P("ctx", None), P("row", None), P("row")),
        out_specs=P("row", "ctx"),
        check_vma=False,
    )
```

time: 106 us -> 66.7 us (0.63)
  waiting for transfers between devices: 46.3 us -> 25.4 us
  local copies, waits for them, and re-layouts: 15 us -> 1.44 us
  starting transfers between devices: 16.5 us -> 11.1 us
  matrix products: 9.4 us -> 10.7 us
    all_to_all x3 -> x2, waiting for transfers between devices: 46.3 us -> 25.4 us  [the longest x1 25.1 us: local(): part_in = lax.all_to_all(part_low, 'ctx', 0, 0, tiled=True)]
    reshape x2 -> x0, local copies, waits for them, and re-layouts: 11.6 us -> none  [the longest x1 10 us: local(): seg_out.reshape(row_count, 1, HEADS * HEAD_DIM)]
    all_to_all x3 -> x2, starting transfers between devices: 16.5 us -> 11.1 us  [the longest x1 6.32 us: local(): stats_in = lax.all_to_all(stats, 'ctx', 0, 0, tiled=True)]
    reduce_sum x2, other arithmetic: 2.07 us -> 0.75 us  [the longest x1 0.72 us: local(): jnp.sum(part_in.astype(jnp.float32) * weight[:, :, :, None], axis=0)]
    broadcast_in_dim x2 -> x0, local copies, waits for them, and re-layouts: 1.22 us -> none  [the longest x1 0.62 us: local(): jnp.transpose(seg_total)[:, None, :]]
    dot_general x1, matrix products: 4.2 us -> 5.34 us  [segment_parts(): jnp.einsum('hqk,khd->hqd', probs_low, value_heads, preferred_element_type...]
  transfers between devices with their start and end apart: 3 -> 2, of which waited for: 1 -> 2; matrix products, arithmetic and copies ran while one was open for 20% -> 8% of each run, Pallas kernels for 0% -> 0%
where the time goes in v1:
time: 66.7 us; the launch traced here: 66.3 us
  waiting for transfers between devices  25.4 us (38%)
  starting transfers between devices  11.1 us (17%)
  matrix products  10.7 us (16%)
  blocking collectives  10.5 us (16%)
  other arithmetic  7.14 us (11%)
  local copies, waits for them, and re-layouts  1.44 us (2%)
    all_to_all x1, waiting for transfers between devices, local(): part_in = lax.all_to_all(part_low, 'ctx', 0, 0, tiled=True)  25.1 us
    all_to_all x1, blocking collectives, local(): regrouped = lax.all_to_all(grouped, 'row', 0, 0, tiled=True)  10.5 us
    all_to_all x1, starting transfers between devices, local(): stats_in = lax.all_to_all(stats, 'ctx', 0, 0, tiled=True)  6.32 us
    dot_general x1, matrix products, segment_parts(): jnp.einsum('hqk,khd->hqd', probs_low, value_heads, preferred_element_type...  5.34 us
    dot_general x1, matrix products, segment_parts(): jnp.einsum('qhd,khd->hqk', query_heads, key_heads, preferred_element_type...  5.32 us
    all_to_all x1, starting transfers between devices, local(): part_in = lax.all_to_all(part_low, 'ctx', 0, 0, tiled=True)  4.78 us
    reduce_sum x1, other arithmetic, segment_parts(): seg_total = jnp.sum(probs_live, axis=2)  3.84 us
  transfers between devices with their start and end apart: 2, of which 2 were waited for; matrix products, arithmetic and copies ran while one was open for 8% of the time, Pallas kernels for 0%

profile of v1, /device:TPU:0, one launch (start us, length us, event | category | flops | bytes accessed | tf_op | source)
XLA Modules:
  0.0 66.3 jit_solution(5003091998495342761)
XLA Ops:
  0.0 0.0 copy-start
  0.0 0.8 %iota_compare_fusion = pred[2,8]{1,0:T(4,128)(4,1)S(1)} fusion(s32[2]{0:T(128)} %param.9), kind=kLoop, calls=%fused_computation.29 | loop fusion | flops 16 | bytes 24 | tf_op jit(solution)/shard_map/lt | solution.py:15
  0.9 0.9 %and_reduce_fusion = pred[2,3]{1,0:T(4,128)(4,1)S(1)} fusion(s32[2,8]{1,0:T(2,128)} %param.8, pred[2,8]{1,0:T(4,128)(4,1)S(1)} %iota_compare_fusion, s32[3]{0:T(128)S(1)} %iota_add_fusion), kind=kLoop, calls=%fused_computation.27 | loop fusion | flops 138 | bytes 98 | tf_op jit(solution)/shard_map/reduce_or | solution.py:18
  1.7 0.1 broadcast_bitcast_fusion
  1.8 0.2 copy.25
  2.0 0.0 copy-done
  2.0 0.0 copy-start.1
  2.1 5.3 %select_reduce_fusion = (f32[16,256]{1,0:T(8,128)S(1)}, f32[16,256,384]{2,1,0:T(8,128)}) fusion(pred[256,384]{1,0:T(8,128)(4,1)S(1)} %copy.25, bf16[384,2048]{1,0:T(8,128)(2,1)S(1)} %copy-done, bf16[256,2048]{1,0:T(8,128)(2,1)} %param.5), kind=kOutput, calls=%fused_computation.1 | convolution fusion | flops 407367680 | bytes 9027584 | tf_op jit(solution)/shard_map/qhd,khd->hqk/dot_general | solution.py:25
  7.4 3.8 %fusion = f32[16,256]{1,0:T(8,128)S(1)} fusion(f32[16,256,384]{2,1,0:T(8,128)} %get-tuple-element.8, f32[16,256]{1,0:T(8,128)S(1)} %get-tuple-element.7, pred[256,384]{1,0:T(8,128)(4,1)S(1)} %copy.25), kind=kLoop, calls=%fused_computation.2 | loop fusion | flops 6287360 | bytes 6422528 | tf_op jit(solution)/shard_map/reduce_sum | solution.py:30
  11.2 0.6 pad_maximum_fusion
  11.9 6.3 %all-to-all-start.1 = ((f32[4,2,4,256]{3,2,1,0:T(4,128)}), f32[4,2,4,256]{3,2,1,0:T(4,128)S(1)}, u32[]{:S(2)}, u32[]{:S(2)}) async-start(f32[4,2,4,256]{3,2,1,0:T(4,128)} %pad_maximum_fusion), calls=%async_computation.1 | async-start | bytes 65536 | tf_op jit(solution)/shard_map/all_to_all | solution.py:55
  18.2 0.0 copy-done.1
  18.2 5.3 %fusion.13 = bf16[16,256,128]{2,1,0:T(8,128)(2,1)} fusion(f32[16,256,384]{2,1,0:T(8,128)} %get-tuple-element.8, f32[16,256]{1,0:T(8,128)S(1)} %get-tuple-element.7, pred[256,384]{1,0:T(8,128)(4,1)S(1)} %copy.25, bf16[384,2048]{1,0:T(8,128)(2,1)S(1)} %copy-done.1), kind=kOutput, calls=%fused_computation.15 | convolution fusion | flops 409468928 | bytes 9027584 | tf_op jit(solution)/shard_map/hqk,khd->hqd/dot_general | solution.py:32
  23.5 0.3 all-to-all-done.1
  23.9 4.8 %all-to-all-start = ((bf16[4,4,256,128]{3,2,1,0:T(8,128)(2,1)}), bf16[4,4,256,128]{3,2,1,0:T(8,128)(2,1)S(1)}, u32[]{:S(2)}, u32[]{:S(2)}) async-start(bf16[4,4,256,128]{3,2,1,0:T(8,128)(2,1)} %bitcast.52), calls=%async_computation | async-start | bytes 2097152 | tf_op jit(solution)/shard_map/all_to_all | solution.py:56
  28.7 25.1 %all-to-all-done = bf16[4,4,256,128]{3,2,1,0:T(8,128)(2,1)S(1)} async-done(((bf16[4,4,256,128]{3,2,1,0:T(8,128)(2,1)}), bf16[4,4,256,128]{3,2,1,0:T(8,128)(2,1)S(1)}, u32[]{:S(2)}, u32[]{:S(2)}) %all-to-all-start) | async-done | bytes 1048608 | tf_op jit(solution)/shard_map/all_to_all | solution.py:56
  53.8 0.7 %multiply_reduce_fusion = f32[4,256,128]{2,1,0:T(8,128)S(1)} fusion(bf16[4,4,256,128]{3,2,1,0:T(8,128)(2,1)S(1)} %all-to-all-done, f32[4,4,256]{2,1,0:T(4,128)S(1)} %get-tuple-element.6), kind=kLoop, calls=%fused_computation.9 | loop fusion | flops 1441792 | bytes 1589248 | tf_op jit(solution)/shard_map/reduce_sum | solution.py:62
  54.5 0.2 fusion.20
  54.7 0.2 copy.30
  55.0 0.1 convert_element_type.20
  55.1 0.1 copy.31
  55.2 10.5 %all_to_all.15 = bf16[8,32,512]{2,1,0:T(8,128)(2,1)S(1)} all-to-all(bf16[8,32,512]{2,1,0:T(8,128)(2,1)S(1)} %copy.31), channel_id=1, replica_groups=mesh['ctx'=4,'row'=8] {'row'}, dimensions={0} | all-to-all | bytes 524288 | tf_op jit(solution)/shard_map/all_to_all | solution.py:68
  65.6 0.7 %copy.55 = bf16[256,512]{1,0:T(8,128)(2,1)} copy(bf16[256,512]{1,0:T(8,128)(2,1)S(1)} %bitcast.54) | data formatting | bytes 524288
  (6 shorter events, 0.1 us)
Async XLA Ops:
  0.0 2.0 %copy-start = (bf16[384,2048]{1,0:T(8,128)(2,1)S(1)}, bf16[384,2048]{1,0:T(8,128)(2,1)}, u32[]{:S(2)}) copy-start(bf16[384,2048]{1,0:T(8,128)(2,1)} %param.6) | copy-start | bytes 4718596
  2.0 16.1 %copy-start.1 = (bf16[384,2048]{1,0:T(8,128)(2,1)S(1)}, bf16[384,2048]{1,0:T(8,128)(2,1)}, u32[]{:S(2)}) copy-start(bf16[384,2048]{1,0:T(8,128)(2,1)} %param.7) | copy-start | bytes 4718596
  11.9 12.0 %all-to-all-start.1 = ((f32[4,2,4,256]{3,2,1,0:T(4,128)}), f32[4,2,4,256]{3,2,1,0:T(4,128)S(1)}, u32[]{:S(2)}, u32[]{:S(2)}) async-start(f32[4,2,4,256]{3,2,1,0:T(4,128)} %pad_maximum_fusion), calls=%async_computation.1 | async-start | bytes 65536 | tf_op jit(solution)/shard_map/all_to_all | solution.py:55
  23.9 29.9 %all-to-all-start = ((bf16[4,4,256,128]{3,2,1,0:T(8,128)(2,1)}), bf16[4,4,256,128]{3,2,1,0:T(8,128)(2,1)S(1)}, u32[]{:S(2)}, u32[]{:S(2)}) async-start(bf16[4,4,256,128]{3,2,1,0:T(8,128)(2,1)} %bitcast.52), calls=%async_computation | async-start | bytes 2097152 | tf_op jit(solution)/shard_map/all_to_all | solution.py:56

commit v2 on v1

--- a/solution.py
+++ b/solution.py
@@ -33,6 +33,19 @@
     return (seg_max, seg_total, seg_out)
 
 
+def split_three(x):
+    hi = lax.reduce_precision(x, exponent_bits=8, mantissa_bits=7)
+    rest = x - hi
+    mid = lax.reduce_precision(rest, exponent_bits=8, mantissa_bits=7)
+    lo = lax.reduce_precision(rest - mid, exponent_bits=8, mantissa_bits=7)
+    return jnp.stack([hi, mid, lo], axis=1).astype(jnp.bfloat16)
+
+
+def join_three(parts):
+    parts = parts.astype(jnp.float32)
+    return (parts[:, 0] + parts[:, 1]) + parts[:, 2]
+
+
 def local(queries, keys, values, block_list, block_count):
     row_count = queries.shape[0]
     ctx_span = keys.shape[0]
@@ -51,9 +64,14 @@
         [seg_max.reshape(shards, head_share, row_count), seg_total.reshape(shards, head_share, row_count)],
         axis=1,
     )
-    part_low = seg_out.astype(jnp.bfloat16).reshape(shards, head_share, row_count, HEAD_DIM)
-    stats_in = lax.all_to_all(stats, "ctx", 0, 0, tiled=True)
-    part_in = lax.all_to_all(part_low, "ctx", 0, 0, tiled=True)
+    part_low = seg_out.astype(jnp.bfloat16).reshape(shards, head_share * row_count, HEAD_DIM)
+    stat_rows = 3 * 2 * head_share * row_count // HEAD_DIM
+    payload = jnp.concatenate(
+        [part_low, split_three(stats).reshape(shards, stat_rows, HEAD_DIM)], axis=1
+    )
+    arrived = lax.all_to_all(payload, "ctx", 0, 0, tiled=True)
+    part_in = arrived[:, : head_share * row_count].reshape(shards, head_share, row_count, HEAD_DIM)
+    stats_in = join_three(arrived[:, head_share * row_count :].reshape(shards, 3, 2, head_share, row_count))
     maxima = stats_in[:, 0]
     totals = stats_in[:, 1]
     row_best = jnp.max(maxima, axis=0)

time: 66.7 us -> 61.2 us (0.918)
  blocking collectives: 10.5 us -> 43.4 us
  waiting for transfers between devices: 25.4 us -> 0 us
  starting transfers between devices: 11.1 us -> 0 us
  matrix products: 10.7 us -> 8.36 us
  local copies, waits for them, and re-layouts: 1.44 us -> 2.19 us
    all_to_all x0 -> x1, blocking collectives: none -> 32.9 us  [local(): arrived = lax.all_to_all(payload, 'ctx', 0, 0, tiled=True)]
    all_to_all x2 -> x0, waiting for transfers between devices: 25.4 us -> none  [the longest x1 25.1 us: local(): part_in = lax.all_to_all(part_low, 'ctx', 0, 0, tiled=True)]
    all_to_all x2 -> x0, starting transfers between devices: 11.1 us -> none  [the longest x1 6.32 us: local(): stats_in = lax.all_to_all(stats, 'ctx', 0, 0, tiled=True)]
    dot_general x1, matrix products: 5.34 us -> 3.16 us  [segment_parts(): jnp.einsum('hqk,khd->hqd', probs_low, value_heads, preferred_element_type...]
    unnamed x5 -> x9, local copies, waits for them, and re-layouts: 0.71 us -> 1.36 us
  transfers between devices with their start and end apart: 2 -> 0, of which waited for: 2 -> 0; matrix products, arithmetic and copies ran while one was open for 8% -> 0% of each run, Pallas kernels for 0% -> 0%
where the time goes in v2:
time: 61.2 us; the launch traced here: 60.9 us
  blocking collectives  43.4 us (71%)
  matrix products  8.36 us (14%)
  other arithmetic  6.86 us (11%)
  local copies, waits for them, and re-layouts  2.19 us (4%)
    all_to_all x1, blocking collectives, local(): arrived = lax.all_to_all(payload, 'ctx', 0, 0, tiled=True)  32.9 us
    all_to_all x1, blocking collectives, local(): regrouped = lax.all_to_all(grouped, 'row', 0, 0, tiled=True)  10.5 us
    dot_general x1, matrix products, segment_parts(): jnp.einsum('qhd,khd->hqk', query_heads, key_heads, preferred_element_type...  5.2 us
    reduce_sum x1, other arithmetic, segment_parts(): seg_total = jnp.sum(probs_live, axis=2)  4 us
    dot_general x1, matrix products, segment_parts(): jnp.einsum('hqk,khd->hqd', probs_low, value_heads, preferred_element_type...  3.16 us
    unnamed x9, local copies, waits for them, and re-layouts  1.36 us

profile of v2, /device:TPU:0, one launch (start us, length us, event | category | flops | bytes accessed | tf_op | source)
XLA Modules:
  0.0 60.9 jit_solution(14424924317648640603)
XLA Ops:
  0.0 0.0 copy-start
  0.0 0.8 %iota_compare_fusion = pred[2,8]{1,0:T(4,128)(4,1)S(1)} fusion(s32[2]{0:T(128)} %param.9), kind=kLoop, calls=%fused_computation.43 | loop fusion | flops 16 | bytes 24 | tf_op jit(solution)/shard_map/lt | solution.py:15
  0.9 0.9 %and_reduce_fusion = pred[2,3]{1,0:T(4,128)(4,1)S(1)} fusion(s32[2,8]{1,0:T(2,128)} %param.8, pred[2,8]{1,0:T(4,128)(4,1)S(1)} %iota_compare_fusion, s32[3]{0:T(128)S(1)} %iota_add_fusion), kind=kLoop, calls=%fused_computation.41 | loop fusion | flops 138 | bytes 98 | tf_op jit(solution)/shard_map/reduce_or | solution.py:18
  1.7 0.1 broadcast_bitcast_fusion
  1.8 0.2 copy.33
  2.0 0.0 copy-done
  2.0 5.2 %select_reduce_fusion = (f32[16,256]{1,0:T(8,128)S(1)}, f32[16,256,384]{2,1,0:T(8,128)}) fusion(pred[256,384]{1,0:T(8,128)(4,1)S(1)} %copy.33, bf16[384,2048]{1,0:T(8,128)(2,1)S(1)} %copy-done, bf16[256,2048]{1,0:T(8,128)(2,1)} %param.5), kind=kOutput, calls=%fused_computation.1 | convolution fusion | flops 407367680 | bytes 9027584 | tf_op jit(solution)/shard_map/qhd,khd->hqk/dot_general | solution.py:25
  7.3 0.0 copy-start.1
  7.3 4.0 %fusion = f32[16,256]{1,0:T(8,128)S(1)} fusion(f32[16,256,384]{2,1,0:T(8,128)} %get-tuple-element.9, f32[16,256]{1,0:T(8,128)S(1)} %get-tuple-element.8, pred[256,384]{1,0:T(8,128)(4,1)S(1)} %copy.33), kind=kLoop, calls=%fused_computation.2 | loop fusion | flops 6287360 | bytes 6422528 | tf_op jit(solution)/shard_map/reduce_sum | solution.py:30
  11.3 0.6 %copy-done.1 = f32[16,256,384]{2,1,0:T(8,128)S(1)} copy-done((f32[16,256,384]{2,1,0:T(8,128)S(1)}, f32[16,256,384]{2,1,0:T(8,128)}, u32[]{:S(2)}) %copy-start.1) | copy-done | bytes 6291480
  11.9 3.2 %fusion.13 = bf16[16,256,128]{2,1,0:T(8,128)(2,1)S(1)} fusion(f32[16,256,384]{2,1,0:T(8,128)S(1)} %copy-done.1, f32[16,256]{1,0:T(8,128)S(1)} %get-tuple-element.8, pred[256,384]{1,0:T(8,128)(4,1)S(1)} %copy.33, bf16[384,2048]{1,0:T(8,128)(2,1)} %param.7), kind=kOutput, calls=%fused_computation.15 | convolution fusion | flops 409468928 | bytes 9027584 | tf_op jit(solution)/shard_map/hqk,khd->hqd/dot_general | solution.py:32
  15.2 0.1 pad_maximum_fusion
  15.3 32.9 %all_to_all.10 = bf16[4,1072,128]{2,1,0:T(8,128)(2,1)S(1)} all-to-all(bf16[4,1072,128]{2,1,0:T(8,128)(2,1)S(1)} %pad_maximum_fusion), channel_id=1, replica_groups=mesh['ctx'=4,'row'=8] {'ctx'}, dimensions={0} | all-to-all | bytes 2195456 | tf_op jit(solution)/shard_map/all_to_all | solution.py:72
  48.4 0.7 %multiply_reduce_fusion = f32[1024,128]{1,0:T(8,128)S(1)} fusion(bf16[4,1072,128]{2,1,0:T(8,128)(2,1)S(1)} %all_to_all.10, f32[4,1024]{1,0:T(4,128)S(1)} %subtract_exponential_fusion), kind=kLoop, calls=%fused_computation.9 | loop fusion | flops 1441792 | bytes 1589248 | tf_op jit(solution)/shard_map/reduce_sum | solution.py:80
  49.2 0.2 divide_convert_fusion
  49.4 0.2 copy.39
  49.6 0.1 convert_element_type.35
  49.7 0.1 copy.40
  49.8 10.5 %all_to_all.11 = bf16[8,32,512]{2,1,0:T(8,128)(2,1)S(1)} all-to-all(bf16[8,32,512]{2,1,0:T(8,128)(2,1)S(1)} %copy.40), channel_id=1, replica_groups=mesh['ctx'=4,'row'=8] {'row'}, dimensions={0} | all-to-all | bytes 524288 | tf_op jit(solution)/shard_map/all_to_all | solution.py:86
  60.2 0.7 %copy.67 = bf16[256,512]{1,0:T(8,128)(2,1)} copy(bf16[256,512]{1,0:T(8,128)(2,1)S(1)} %bitcast.64) | data formatting | bytes 524288
  (19 shorter events, 0.3 us)
Async XLA Ops:
  0.0 2.0 %copy-start = (bf16[384,2048]{1,0:T(8,128)(2,1)S(1)}, bf16[384,2048]{1,0:T(8,128)(2,1)}, u32[]{:S(2)}) copy-start(bf16[384,2048]{1,0:T(8,128)(2,1)} %param.6) | copy-start | bytes 4718596
  7.3 4.6 %copy-start.1 = (f32[16,256,384]{2,1,0:T(8,128)S(1)}, f32[16,256,384]{2,1,0:T(8,128)}, u32[]{:S(2)}) copy-start(f32[16,256,384]{2,1,0:T(8,128)} %get-tuple-element.9) | copy-start | bytes 18874372

commit v3 on v2

--- a/solution.py
+++ b/solution.py
@@ -60,31 +60,37 @@
         values.reshape(ctx_span, HEADS, HEAD_DIM),
         chosen,
     )
-    stats = jnp.stack(
-        [seg_max.reshape(shards, head_share, row_count), seg_total.reshape(shards, head_share, row_count)],
-        axis=1,
-    )
-    part_low = seg_out.astype(jnp.bfloat16).reshape(shards, head_share * row_count, HEAD_DIM)
-    stat_rows = 3 * 2 * head_share * row_count // HEAD_DIM
-    payload = jnp.concatenate(
-        [part_low, split_three(stats).reshape(shards, stat_rows, HEAD_DIM)], axis=1
-    )
-    arrived = lax.all_to_all(payload, "ctx", 0, 0, tiled=True)
-    part_in = arrived[:, : head_share * row_count].reshape(shards, head_share, row_count, HEAD_DIM)
-    stats_in = join_three(arrived[:, head_share * row_count :].reshape(shards, 3, 2, head_share, row_count))
-    maxima = stats_in[:, 0]
-    totals = stats_in[:, 1]
-    row_best = jnp.max(maxima, axis=0)
-    weight = jnp.exp(maxima - row_best[None])
-    total_sum = jnp.sum(totals * weight, axis=0)
-    numerator = jnp.sum(part_in.astype(jnp.float32) * weight[:, :, :, None], axis=0)
-    attended = numerator / total_sum[:, :, None]
-    attended_low = jnp.transpose(attended, (1, 0, 2)).reshape(row_count, share_width).astype(jnp.bfloat16)
     owners = lax.axis_size("row")
     per_owner = row_count // owners
-    grouped = jnp.transpose(attended_low.reshape(per_owner, owners, share_width), (1, 0, 2))
-    regrouped = lax.all_to_all(grouped, "row", 0, 0, tiled=True)
-    return regrouped.reshape(row_count, share_width)
+    part_low = seg_out.astype(jnp.bfloat16).reshape(shards, head_share, per_owner, owners, HEAD_DIM)
+    part_low = jnp.transpose(part_low, (3, 0, 1, 2, 4)).reshape(
+        owners * shards, head_share * per_owner, HEAD_DIM
+    )
+    stats = jnp.stack([seg_max, seg_total]).reshape(2, shards, head_share, per_owner, owners)
+    stats = jnp.transpose(stats, (4, 1, 0, 2, 3)).reshape(owners * shards, 2, head_share, per_owner)
+    stat_count = 3 * 2 * head_share * per_owner
+    stat_rows = -(-stat_count // HEAD_DIM)
+    stat_low = split_three(stats).reshape(owners * shards, stat_count)
+    stat_low = jnp.pad(stat_low, ((0, 0), (0, stat_rows * HEAD_DIM - stat_count)))
+    payload = jnp.concatenate(
+        [part_low, stat_low.reshape(owners * shards, stat_rows, HEAD_DIM)], axis=1
+    )
+    arrived = lax.all_to_all(payload, ("row", "ctx"), 0, 0, tiled=True)
+    arrived = arrived.reshape(owners, shards, head_share * per_owner + stat_rows, HEAD_DIM)
+    part_in = arrived[:, :, : head_share * per_owner].reshape(owners, shards, head_share, per_owner, HEAD_DIM)
+    stat_in = arrived[:, :, head_share * per_owner :].reshape(owners * shards, stat_rows * HEAD_DIM)
+    stats_in = join_three(
+        stat_in[:, :stat_count].reshape(owners * shards, 3, 2, head_share, per_owner)
+    ).reshape(owners, shards, 2, head_share, per_owner)
+    maxima = stats_in[:, :, 0]
+    totals = stats_in[:, :, 1]
+    row_best = jnp.max(maxima, axis=1)
+    weight = jnp.exp(maxima - row_best[:, None])
+    total_sum = jnp.sum(totals * weight, axis=1)
+    numerator = jnp.sum(part_in.astype(jnp.float32) * weight[..., None], axis=1)
+    attended = numerator / total_sum[..., None]
+    attended_low = jnp.transpose(attended, (0, 2, 1, 3)).reshape(row_count, share_width)
+    return attended_low.astype(jnp.bfloat16)
 
 
 def solution(mesh):

time: 61.2 us -> 55.4 us (0.905)
  blocking collectives: 43.4 us -> 36.3 us
  local copies, waits for them, and re-layouts: 2.19 us -> 3.4 us
    all_to_all x2 -> x1, blocking collectives: 43.4 us -> 36.3 us  [local(): arrived = lax.all_to_all(payload, ('row', 'ctx'), 0, 0, tiled=True)]
    unnamed x9 -> x6, local copies, waits for them, and re-layouts: 1.36 us -> 1.4 us
where the time goes in v3:
time: 55.4 us; the launch traced here: 55.2 us
  blocking collectives  36.3 us (66%)
  matrix products  8.36 us (15%)
  other arithmetic  6.99 us (13%)
  local copies, waits for them, and re-layouts  3.4 us (6%)
    all_to_all x1, blocking collectives, local(): arrived = lax.all_to_all(payload, ('row', 'ctx'), 0, 0, tiled=True)  36.3 us
    dot_general x1, matrix products, segment_parts(): jnp.einsum('qhd,khd->hqk', query_heads, key_heads, preferred_element_type...  5.2 us
    reduce_sum x1, other arithmetic, segment_parts(): seg_total = jnp.sum(probs_live, axis=2)  4 us
    dot_general x1, matrix products, segment_parts(): jnp.einsum('hqk,khd->hqd', probs_low, value_heads, preferred_element_type...  3.16 us
    unnamed x6, local copies, waits for them, and re-layouts  1.4 us

profile of v3, /device:TPU:0, one launch (start us, length us, event | category | flops | bytes accessed | tf_op | source)
XLA Modules:
  0.0 55.2 jit_solution(4789024152158359047)
XLA Ops:
  0.0 0.0 copy-start
  0.0 0.8 %iota_compare_fusion = pred[2,8]{1,0:T(4,128)(4,1)S(1)} fusion(s32[2]{0:T(128)} %param.9), kind=kLoop, calls=%fused_computation.40 | loop fusion | flops 16 | bytes 24 | tf_op jit(solution)/shard_map/lt | solution.py:15
  0.9 0.9 %and_reduce_fusion = pred[2,3]{1,0:T(4,128)(4,1)S(1)} fusion(s32[2,8]{1,0:T(2,128)} %param.8, pred[2,8]{1,0:T(4,128)(4,1)S(1)} %iota_compare_fusion, s32[3]{0:T(128)S(1)} %iota_add_fusion), kind=kLoop, calls=%fused_computation.38 | loop fusion | flops 138 | bytes 98 | tf_op jit(solution)/shard_map/reduce_or | solution.py:18
  1.7 0.1 broadcast_bitcast_fusion
  1.8 0.2 copy.41
  2.0 0.0 copy-done
  2.0 5.2 %select_reduce_fusion = (f32[16,256]{1,0:T(8,128)S(1)}, f32[16,256,384]{2,1,0:T(8,128)}) fusion(pred[256,384]{1,0:T(8,128)(4,1)S(1)} %copy.41, bf16[384,2048]{1,0:T(8,128)(2,1)S(1)} %copy-done, bf16[256,2048]{1,0:T(8,128)(2,1)} %param.5), kind=kOutput, calls=%fused_computation.1 | convolution fusion | flops 407367680 | bytes 9027584 | tf_op jit(solution)/shard_map/qhd,khd->hqk/dot_general | solution.py:25
  7.2 0.2 stack.16
  7.4 0.0 copy-start.1
  7.4 4.0 %fusion = f32[16,256]{1,0:T(8,128)S(1)} fusion(f32[16,256,384]{2,1,0:T(8,128)} %get-tuple-element.11, f32[16,256]{1,0:T(8,128)S(1)} %get-tuple-element.10, pred[256,384]{1,0:T(8,128)(4,1)S(1)} %copy.41), kind=kLoop, calls=%fused_computation.2 | loop fusion | flops 6287360 | bytes 6422528 | tf_op jit(solution)/shard_map/reduce_sum | solution.py:30
  11.4 0.6 %copy-done.1 = f32[16,256,384]{2,1,0:T(8,128)S(1)} copy-done((f32[16,256,384]{2,1,0:T(8,128)S(1)}, f32[16,256,384]{2,1,0:T(8,128)}, u32[]{:S(2)}) %copy-start.1) | copy-done | bytes 6291480
  12.1 3.2 %fusion.13 = bf16[16,256,128]{2,1,0:T(8,128)(2,1)S(1)} fusion(f32[16,256,384]{2,1,0:T(8,128)S(1)} %copy-done.1, f32[16,256]{1,0:T(8,128)S(1)} %get-tuple-element.10, pred[256,384]{1,0:T(8,128)(4,1)S(1)} %copy.41, bf16[384,2048]{1,0:T(8,128)(2,1)} %param.7), kind=kOutput, calls=%fused_computation.15 | convolution fusion | flops 409468928 | bytes 9027584 | tf_op jit(solution)/shard_map/hqk,khd->hqd/dot_general | solution.py:32
  15.2 0.2 copy.45
  15.5 0.1 copy.46
  15.6 0.2 stack.17
  15.8 0.1 copy.47
  15.9 0.1 copy.48
  16.1 0.1 copy.53
  16.2 0.1 reshape.133
  16.4 0.1 pad_maximum_fusion
  16.5 36.3 %all_to_all.5 = bf16[32,134,128]{2,1,0:T(8,128)(2,1)S(1)} all-to-all(bf16[32,134,128]{2,1,0:T(8,128)(2,1)S(1)} %pad_maximum_fusion), channel_id=1, replica_groups=mesh['ctx'=4,'row'=8] {'row','ctx'}, dimensions={0} | all-to-all | bytes 2195456 | tf_op jit(solution)/shard_map/all_to_all | solution.py:78
  52.8 0.2 reshape.132
  53.2 0.1 sub.54
  53.2 0.1 squeeze.11
  53.4 0.7 %multiply_reduce_fusion = f32[8,128,128]{2,1,0:T(8,128)S(1)} fusion(bf16[8,4,134,128]{3,2,1,0:T(8,128)(2,1)S(1)} %bitcast.65, f32[8,4,128]{2,1,0:T(4,128)S(1)} %subtract_exponential_fusion), kind=kLoop, calls=%fused_computation.9 | loop fusion | flops 1441792 | bytes 1589248 | tf_op jit(solution)/shard_map/reduce_sum | solution.py:90
  54.1 0.2 divide_convert_fusion
  54.3 0.1 copy.52
  54.5 0.7 %copy.80 = bf16[32,8,4,128]{3,1,2,0:T(8,128)(2,1)} copy(bf16[32,8,4,128]{3,2,1,0:T(4,128)(2,1)S(1)} %bitcast.69) | data formatting | bytes 524288
  (11 shorter events, 0.3 us)
Async XLA Ops:
  0.0 2.0 %copy-start = (bf16[384,2048]{1,0:T(8,128)(2,1)S(1)}, bf16[384,2048]{1,0:T(8,128)(2,1)}, u32[]{:S(2)}) copy-start(bf16[384,2048]{1,0:T(8,128)(2,1)} %param.6) | copy-start | bytes 4718596
  7.4 4.6 %copy-start.1 = (f32[16,256,384]{2,1,0:T(8,128)S(1)}, f32[16,256,384]{2,1,0:T(8,128)}, u32[]{:S(2)}) copy-start(f32[16,256,384]{2,1,0:T(8,128)} %get-tuple-element.11) | copy-start | bytes 18874372

commit v4 on v3

v4 whole, which is shorter than its diff:
```python
import functools

import jax
import jax.numpy as jnp
from jax import lax
from jax.experimental import pallas as pl
from jax.experimental.pallas import tpu as pltpu
from jax.sharding import PartitionSpec as P

HEADS = 16
HEAD_DIM = 128
BLOCK = 128


masked_fill = -1e30


def attention_kernel(shape, list_ref, count_ref, first_ref, q_ref, k_ref, v_ref, part_ref, stat_ref,
                     bias_ref, any_ref):
    owners, per_owner, head_share, q_blocks, k_blocks, max_sel = shape
    rows = owners * per_owner

    @pl.when(pl.program_id(0) == 0)
    def _():
        first = first_ref[0]
        pos = lax.broadcasted_iota(jnp.int32, (rows, 1), 0)
        frame = (pos % per_owner) * owners + pos // per_owner
        q_block = frame // BLOCK
        any_live = jnp.zeros((rows, 1), jnp.int32)
        for b in range(k_blocks):
            live = jnp.zeros((rows, 1), jnp.int32)
            for a in range(q_blocks):
                hit = jnp.int32(0)
                for slot in range(max_sel):
                    found = (list_ref[a * max_sel + slot] == first + b) & (slot < count_ref[a])
                    hit = jnp.maximum(hit, jnp.where(found, 1, 0).astype(jnp.int32))
                live = jnp.where(q_block == a, hit, live)
            any_live = jnp.maximum(any_live, live)
            bias = jnp.where(live > 0, 0.0, masked_fill).astype(jnp.float32)
            bias_ref[:, b * BLOCK : (b + 1) * BLOCK] = jnp.broadcast_to(bias, (rows, BLOCK))
        any_ref[...] = jnp.broadcast_to(any_live, (rows, HEAD_DIM))

    score_scale = 1.0 / HEAD_DIM**0.5
    row_live = any_ref[:, 0:1] > 0
    for hl in range(head_share):
        cols = slice(hl * HEAD_DIM, (hl + 1) * HEAD_DIM)
        scores = lax.dot_general(
            q_ref[:, cols], k_ref[:, cols], (((1,), (1,)), ((), ())), preferred_element_type=jnp.float32
        )
        scores = scores * score_scale + bias_ref[...]
        seg_max = jnp.max(scores, axis=1, keepdims=True)
        probs = jnp.exp(scores - seg_max)
        seg_total = jnp.where(row_live, jnp.sum(probs, axis=1, keepdims=True), 0.0)
        seg_out = jnp.dot(probs.astype(jnp.bfloat16), v_ref[:, cols], preferred_element_type=jnp.float32)
        seg_out = jnp.where(row_live, seg_out, 0.0)
        part_ref[:, hl, :, :] = seg_out.reshape(owners, per_owner, HEAD_DIM).astype(jnp.bfloat16)
        stat_ref[hl, :, 0:1] = seg_max
        stat_ref[hl, :, 1:2] = seg_total


def local_attention(queries_perm, keys, values, block_list, block_count, first_block, owners, shards):
    rows = queries_perm.shape[0]
    ctx_span = keys.shape[0]
    per_owner = rows // owners
    head_share = HEADS // shards
    share_width = head_share * HEAD_DIM
    q_blocks = rows // BLOCK
    k_blocks = ctx_span // BLOCK
    max_sel = block_list.shape[1]
    shape = (owners, per_owner, head_share, q_blocks, k_blocks, max_sel)
    grid_spec = pltpu.PrefetchScalarGridSpec(
        num_scalar_prefetch=3,
        grid=(shards,),
        in_specs=[
            pl.BlockSpec((rows, share_width), lambda g, *_: (0, g)),
            pl.BlockSpec((ctx_span, share_width), lambda g, *_: (0, g)),
            pl.BlockSpec((ctx_span, share_width), lambda g, *_: (0, g)),
        ],
        out_specs=[
            pl.BlockSpec((owners, head_share, per_owner, HEAD_DIM), lambda g, *_: (0, g, 0, 0)),
            pl.BlockSpec((head_share, rows, 2), lambda g, *_: (g, 0, 0)),
        ],
        scratch_shapes=[
            pltpu.VMEM((rows, ctx_span), jnp.float32),
            pltpu.VMEM((rows, HEAD_DIM), jnp.int32),
        ],
    )
    flops = 4 * HEADS * rows * ctx_span * HEAD_DIM
    return pl.pallas_call(
        functools.partial(attention_kernel, shape),
        grid_spec=grid_spec,
        out_shape=[
            jax.ShapeDtypeStruct((owners, HEADS, per_owner, HEAD_DIM), jnp.bfloat16),
            jax.ShapeDtypeStruct((HEADS, rows, 2), jnp.float32),
        ],
        compiler_params=pltpu.CompilerParams(dimension_semantics=("arbitrary",)),
        cost_estimate=pl.CostEstimate(
            flops=flops,
            transcendentals=HEADS * rows * ctx_span,
            bytes_accessed=2 * (queries_perm.size + keys.size + values.size) + 2 * rows * HEADS * HEAD_DIM,
        ),
    )(block_list.reshape(-1), block_count, first_block, queries_perm, keys, values)


def split_three(x):
    hi = lax.reduce_precision(x, exponent_bits=8, mantissa_bits=7)
    rest = x - hi
    mid = lax.reduce_precision(rest, exponent_bits=8, mantissa_bits=7)
    lo = lax.reduce_precision(rest - mid, exponent_bits=8, mantissa_bits=7)
    return jnp.stack([hi, mid, lo], axis=1).astype(jnp.bfloat16)


def join_three(parts):
    parts = parts.astype(jnp.float32)
    return (parts[:, 0] + parts[:, 1]) + parts[:, 2]


def local(queries, keys, values, block_list, block_count):
    row_count = queries.shape[0]
    ctx_span = keys.shape[0]
    shards = lax.axis_size("ctx")
    owners = lax.axis_size("row")
    per_owner = row_count // owners
    head_share = HEADS // shards
    share_width = head_share * HEAD_DIM
    blocks_here = ctx_span // BLOCK
    first_block = (lax.axis_index("ctx") * blocks_here).astype(jnp.int32).reshape(1)
    queries_perm = jnp.transpose(queries.reshape(per_owner, owners, -1), (1, 0, 2)).reshape(row_count, -1)
    part, stat = local_attention(
        queries_perm, keys, values, block_list, block_count.astype(jnp.int32), first_block, owners, shards
    )
    part_low = part.reshape(owners * shards, head_share * per_owner, HEAD_DIM)
    stats = jnp.transpose(stat.reshape(shards, head_share, owners, per_owner, 2), (2, 0, 4, 1, 3))
    stats = stats.reshape(owners * shards, 2, head_share, per_owner)
    stat_count = 3 * 2 * head_share * per_owner
    stat_rows = -(-stat_count // HEAD_DIM)
    stat_low = split_three(stats).reshape(owners * shards, stat_count)
    stat_low = jnp.pad(stat_low, ((0, 0), (0, stat_rows * HEAD_DIM - stat_count)))
    payload = jnp.concatenate(
        [part_low, stat_low.reshape(owners * shards, stat_rows, HEAD_DIM)], axis=1
    )
    arrived = lax.all_to_all(payload, ("row", "ctx"), 0, 0, tiled=True)
    arrived = arrived.reshape(owners, shards, head_share * per_owner + stat_rows, HEAD_DIM)
    part_in = arrived[:, :, : head_share * per_owner].reshape(owners, shards, head_share, per_owner, HEAD_DIM)
    stat_in = arrived[:, :, head_share * per_owner :].reshape(owners * shards, stat_rows * HEAD_DIM)
    stats_in = join_three(
        stat_in[:, :stat_count].reshape(owners * shards, 3, 2, head_share, per_owner)
    ).reshape(owners, shards, 2, head_share, per_owner)
    maxima = stats_in[:, :, 0]
    totals = stats_in[:, :, 1]
    row_best = jnp.max(maxima, axis=1)
    weight = jnp.exp(maxima - row_best[:, None])
    total_sum = jnp.sum(totals * weight, axis=1)
    numerator = jnp.sum(part_in.astype(jnp.float32) * weight[..., None], axis=1)
    attended = numerator / total_sum[..., None]
    attended_low = jnp.transpose(attended, (0, 2, 1, 3)).reshape(row_count, share_width)
    return attended_low.astype(jnp.bfloat16)


def solution(mesh):
    return jax.shard_map(
        local,
        mesh=mesh,
        in_specs=(P("row", None), P("ctx", None), P("ctx", None), P("row", None), P("row")),
        out_specs=P("row", "ctx"),
        check_vma=False,
    )
```

time: 55.4 us -> 56.9 us (1.027)
  Pallas kernels: 0 us -> 9.21 us
  matrix products: 8.36 us -> 0 us
  local copies, waits for them, and re-layouts: 3.4 us -> 8.69 us
  other arithmetic: 6.99 us -> 2.39 us
    pallas_call x0 -> x1, Pallas kernels: none -> 9.21 us  [local_attention(): pl.pallas_call(functools.partial(attention_kernel, shape), grid_spec=grid...]
    dot_general x2 -> x0, matrix products: 8.36 us -> none  [the longest x1 5.2 us: segment_parts(): jnp.einsum('qhd,khd->hqk', query_heads, key_heads, preferred_element_type...]
    reshape x2 -> x3, local copies, waits for them, and re-layouts: 0.31 us -> 6.61 us  [the longest x1 2.79 us: local(): queries.reshape(per_owner, owners, -1)]
    reduce_sum x1 -> x0, other arithmetic: 4 us -> none  [segment_parts(): seg_total = jnp.sum(probs_live, axis=2)]
    reduce_sum x1, other arithmetic: 0.73 us -> 1.86 us  [local(): numerator = jnp.sum(part_in.astype(jnp.float32) * weight[..., None], axis=1)]
    reduce_or x1 -> x0, other arithmetic: 0.86 us -> none  [chosen_range(): return jnp.any(block_hits, axis=1)]
    lt x1 -> x0, other arithmetic: 0.84 us -> none  [chosen_range(): jnp.arange(block_list.shape[1], dtype=jnp.int32)[None, :]]
    unnamed x6 -> x3, local copies, waits for them, and re-layouts: 1.4 us -> 0.74 us
where the time goes in v4:
time: 56.9 us; the launch traced here: 56.7 us
  blocking collectives  36.3 us (64%)
  Pallas kernels  9.21 us (16%)
  local copies, waits for them, and re-layouts  8.69 us (15%)
  other arithmetic  2.39 us (4%)
    all_to_all x1, blocking collectives, local(): arrived = lax.all_to_all(payload, ('row', 'ctx'), 0, 0, tiled=True)  36.3 us
    pallas_call x1, Pallas kernels, local_attention(): pl.pallas_call(functools.partial(attention_kernel, shape), grid_spec=grid...  9.21 us
    reshape x1, local copies, waits for them, and re-layouts, local(): queries.reshape(per_owner, owners, -1)  2.79 us
    reshape x1, local copies, waits for them, and re-layouts, local(): stat.reshape(shards, head_share, owners, per_owner, 2)  2.56 us
    reduce_sum x1, other arithmetic, local(): numerator = jnp.sum(part_in.astype(jnp.float32) * weight[..., None], axis=1)  1.86 us
    reshape x1, local copies, waits for them, and re-layouts, local_attention(): block_list.reshape(-1)  1.27 us

profile of v4, /device:TPU:0, one launch (start us, length us, event | category | flops | bytes accessed | tf_op | source)
XLA Modules:
  0.0 56.7 jit_solution(11187623078562889406)
XLA Ops:
  0.0 1.3 %reshape.91.list_ref = s32[16]{0:T(128)} reshape(s32[2,8]{1,0:T(2,128)} %param.8) | data formatting | bytes 128 | tf_op jit(solution)/shard_map/reshape | solution.py:102
  1.3 2.8 %copy.32 = bf16[32,8,2048]{2,0,1:T(8,128)(2,1)} copy(bf16[32,8,2048]{2,1,0:T(8,128)(2,1)} %bitcast.42) | data formatting | bytes 2097152 | tf_op jit(solution)/shard_map/reshape | solution.py:128
  4.1 9.2 %shard_map.55 = (bf16[8,16,32,128]{3,2,1,0:T(8,128)(2,1)}, f32[16,256,2]{2,1,0:T(8,128)}) custom-call(s32[16]{0:T(128)} %reshape.91.list_ref, s32[2]{0:T(128)} %count_ref.1, s32[1]{0:T(128)} %bitcast.first_ref, bf16[256,2048]{1,0:T(8,128)(2,1)} %bitcast.39, bf16[384,2048]{1,0:T(8,128)(2,1)} %k_ref.1, bf16[384,2048]{1,0:T(8,128)(2,1)} %v_ref.1), custom_call_target="tpu_custom_call" | custom-call | flops 805306368 | bytes 5242880 | tf_op jit(solution)/shard_map/pallas_call | solution.py:89
  13.3 0.0 copy-start
  13.3 2.6 %copy.33 = f32[4,4,8,32,2]{3,0,2,1,4:T(4,128)S(1)} copy(f32[4,4,8,32,2]{4,3,2,1,0:T(8,128)} %bitcast.40) | data formatting | bytes 65536 | tf_op jit(solution)/shard_map/reshape | solution.py:133
  15.9 0.1 copy.42
  16.0 0.1 reshape.100
  16.2 0.0 copy-done
  16.2 0.1 pad_maximum_fusion
  16.3 36.3 %all_to_all.5 = bf16[32,134,128]{2,1,0:T(8,128)(2,1)S(1)} all-to-all(bf16[32,134,128]{2,1,0:T(8,128)(2,1)S(1)} %pad_maximum_fusion), channel_id=1, replica_groups=mesh['ctx'=4,'row'=8] {'row','ctx'}, dimensions={0} | all-to-all | bytes 2195456 | tf_op jit(solution)/shard_map/all_to_all | solution.py:142
  52.6 0.2 copy.36
  52.8 0.2 reshape.99
  53.1 0.1 reshape.101
  53.2 0.1 sub.44
  53.3 0.3 copy.38
  53.6 1.9 %multiply_reduce_fusion = f32[8,128,128]{2,0,1:T(8,128)S(1)} fusion(bf16[8,4,134,128]{3,1,0,2:T(4,128)(2,1)S(1)} %bitcast.38, f32[8,4,128]{1,0,2:T(8,128)S(1)} %copy.38), kind=kLoop, calls=%fused_computation | loop fusion | flops 1441792 | bytes 1589248 | tf_op jit(solution)/shard_map/reduce_sum | solution.py:154
  55.5 0.1 copy.39
  55.6 0.2 divide_convert_fusion
  55.8 0.1 copy.41
  55.9 0.7 %copy.57 = bf16[32,8,4,128]{3,1,2,0:T(8,128)(2,1)} copy(bf16[32,8,4,128]{3,2,1,0:T(4,128)(2,1)S(1)} %bitcast.44) | data formatting | bytes 524288
  (7 shorter events, 0.2 us)
Async XLA Ops:
  13.3 2.9 %copy-start = (bf16[8,16,32,128]{3,2,1,0:T(8,128)(2,1)S(1)}, bf16[8,16,32,128]{3,2,1,0:T(8,128)(2,1)}, u32[]{:S(2)}) copy-start(bf16[8,16,32,128]{3,2,1,0:T(8,128)(2,1)} %get-tuple-element.7) | copy-start | bytes 3145732

commit v5 on v4

--- a/solution.py
+++ b/solution.py
@@ -17,31 +17,29 @@
 
 def attention_kernel(shape, list_ref, count_ref, first_ref, q_ref, k_ref, v_ref, part_ref, stat_ref,
                      bias_ref, any_ref):
-    owners, per_owner, head_share, q_blocks, k_blocks, max_sel = shape
-    rows = owners * per_owner
+    rows, head_share, q_blocks, k_blocks, max_sel = shape
 
     @pl.when(pl.program_id(0) == 0)
     def _():
         first = first_ref[0]
-        pos = lax.broadcasted_iota(jnp.int32, (rows, 1), 0)
-        frame = (pos % per_owner) * owners + pos // per_owner
-        q_block = frame // BLOCK
-        any_live = jnp.zeros((rows, 1), jnp.int32)
-        for b in range(k_blocks):
-            live = jnp.zeros((rows, 1), jnp.int32)
-            for a in range(q_blocks):
+        for a in range(q_blocks):
+            any_live = jnp.int32(0)
+            for b in range(k_blocks):
                 hit = jnp.int32(0)
                 for slot in range(max_sel):
-                    found = (list_ref[a * max_sel + slot] == first + b) & (slot < count_ref[a])
+                    found = (list_ref[a, slot] == first + b) & (slot < count_ref[a])
                     hit = jnp.maximum(hit, jnp.where(found, 1, 0).astype(jnp.int32))
-                live = jnp.where(q_block == a, hit, live)
-            any_live = jnp.maximum(any_live, live)
-            bias = jnp.where(live > 0, 0.0, masked_fill).astype(jnp.float32)
-            bias_ref[:, b * BLOCK : (b + 1) * BLOCK] = jnp.broadcast_to(bias, (rows, BLOCK))
-        any_ref[...] = jnp.broadcast_to(any_live, (rows, HEAD_DIM))
+                any_live = jnp.maximum(any_live, hit)
+                bias = jnp.where(hit > 0, 0.0, masked_fill).astype(jnp.float32)
+                bias_ref[a * BLOCK : (a + 1) * BLOCK, b * BLOCK : (b + 1) * BLOCK] = jnp.full(
+                    (BLOCK, BLOCK), bias, jnp.float32
+                )
+            any_ref[a * BLOCK : (a + 1) * BLOCK, :] = jnp.full((BLOCK, HEAD_DIM), any_live, jnp.int32)
 
     score_scale = 1.0 / HEAD_DIM**0.5
     row_live = any_ref[:, 0:1] > 0
+    lane = lax.broadcasted_iota(jnp.int32, (rows, HEAD_DIM), 1)
+    stats = jnp.zeros((rows, HEAD_DIM), jnp.float32)
     for hl in range(head_share):
         cols = slice(hl * HEAD_DIM, (hl + 1) * HEAD_DIM)
         scores = lax.dot_general(
@@ -52,22 +50,21 @@
         probs = jnp.exp(scores - seg_max)
         seg_total = jnp.where(row_live, jnp.sum(probs, axis=1, keepdims=True), 0.0)
         seg_out = jnp.dot(probs.astype(jnp.bfloat16), v_ref[:, cols], preferred_element_type=jnp.float32)
-        seg_out = jnp.where(row_live, seg_out, 0.0)
-        part_ref[:, hl, :, :] = seg_out.reshape(owners, per_owner, HEAD_DIM).astype(jnp.bfloat16)
-        stat_ref[hl, :, 0:1] = seg_max
-        stat_ref[hl, :, 1:2] = seg_total
+        part_ref[hl] = jnp.where(row_live, seg_out, 0.0).astype(jnp.bfloat16)
+        stats = jnp.where(lane == hl, seg_max, stats)
+        stats = jnp.where(lane == head_share + hl, seg_total, stats)
+    stat_ref[0] = jnp.transpose(stats)[: 2 * head_share]
 
 
-def local_attention(queries_perm, keys, values, block_list, block_count, first_block, owners, shards):
-    rows = queries_perm.shape[0]
+def local_attention(queries, keys, values, block_list, block_count, first_block, shards):
+    rows = queries.shape[0]
     ctx_span = keys.shape[0]
-    per_owner = rows // owners
     head_share = HEADS // shards
     share_width = head_share * HEAD_DIM
     q_blocks = rows // BLOCK
     k_blocks = ctx_span // BLOCK
     max_sel = block_list.shape[1]
-    shape = (owners, per_owner, head_share, q_blocks, k_blocks, max_sel)
+    shape = (rows, head_share, q_blocks, k_blocks, max_sel)
     grid_spec = pltpu.PrefetchScalarGridSpec(
         num_scalar_prefetch=3,
         grid=(shards,),
@@ -77,8 +74,8 @@
             pl.BlockSpec((ctx_span, share_width), lambda g, *_: (0, g)),
         ],
         out_specs=[
-            pl.BlockSpec((owners, head_share, per_owner, HEAD_DIM), lambda g, *_: (0, g, 0, 0)),
-            pl.BlockSpec((head_share, rows, 2), lambda g, *_: (g, 0, 0)),
+            pl.BlockSpec((head_share, rows, HEAD_DIM), lambda g, *_: (g, 0, 0)),
+            pl.BlockSpec((1, 2 * head_share, rows), lambda g, *_: (g, 0, 0)),
         ],
         scratch_shapes=[
             pltpu.VMEM((rows, ctx_span), jnp.float32),
@@ -90,16 +87,16 @@
         functools.partial(attention_kernel, shape),
         grid_spec=grid_spec,
         out_shape=[
-            jax.ShapeDtypeStruct((owners, HEADS, per_owner, HEAD_DIM), jnp.bfloat16),
-            jax.ShapeDtypeStruct((HEADS, rows, 2), jnp.float32),
+            jax.ShapeDtypeStruct((HEADS, rows, HEAD_DIM), jnp.bfloat16),
+            jax.ShapeDtypeStruct((shards, 2 * head_share, rows), jnp.float32),
         ],
         compiler_params=pltpu.CompilerParams(dimension_semantics=("arbitrary",)),
         cost_estimate=pl.CostEstimate(
             flops=flops,
             transcendentals=HEADS * rows * ctx_span,
-            bytes_accessed=2 * (queries_perm.size + keys.size + values.size) + 2 * rows * HEADS * HEAD_DIM,
+            bytes_accessed=2 * (queries.size + keys.size + values.size) + 2 * rows * HEADS * HEAD_DIM,
         ),
-    )(block_list.reshape(-1), block_count, first_block, queries_perm, keys, values)
+    )(block_list, block_count, first_block, queries, keys, values)
 
 
 def split_three(x):
@@ -125,12 +122,14 @@
     share_width = head_share * HEAD_DIM
     blocks_here = ctx_span // BLOCK
     first_block = (lax.axis_index("ctx") * blocks_here).astype(jnp.int32).reshape(1)
-    queries_perm = jnp.transpose(queries.reshape(per_owner, owners, -1), (1, 0, 2)).reshape(row_count, -1)
     part, stat = local_attention(
-        queries_perm, keys, values, block_list, block_count.astype(jnp.int32), first_block, owners, shards
+        queries, keys, values, block_list.astype(jnp.int32), block_count.astype(jnp.int32), first_block, shards
     )
-    part_low = part.reshape(owners * shards, head_share * per_owner, HEAD_DIM)
-    stats = jnp.transpose(stat.reshape(shards, head_share, owners, per_owner, 2), (2, 0, 4, 1, 3))
+    part_low = part.reshape(shards, head_share, per_owner, owners, HEAD_DIM)
+    part_low = jnp.transpose(part_low, (3, 0, 1, 2, 4)).reshape(
+        owners * shards, head_share * per_owner, HEAD_DIM
+    )
+    stats = jnp.transpose(stat.reshape(shards, 2, head_share, per_owner, owners), (4, 0, 1, 2, 3))
     stats = stats.reshape(owners * shards, 2, head_share, per_owner)
     stat_count = 3 * 2 * head_share * per_owner
     stat_rows = -(-stat_count // HEAD_DIM)

time: 56.9 us -> 50.3 us (0.88)
  local copies, waits for them, and re-layouts: 8.69 us -> 3.54 us
  other arithmetic: 2.39 us -> 1.27 us
    reshape x3 -> x2, local copies, waits for them, and re-layouts: 6.61 us -> 1.77 us  [the longest x1 1.47 us: local(): part_low = part.reshape(shards, head_share, per_owner, owners, HEAD_DIM)]
    reduce_sum x1, other arithmetic: 1.86 us -> 0.73 us  [local(): numerator = jnp.sum(part_in.astype(jnp.float32) * weight[..., None], axis=1)]
where the time goes in v5:
time: 50.3 us; the launch traced here: 50.1 us
  blocking collectives  36.3 us (72%)
  Pallas kernels  8.93 us (18%)
  local copies, waits for them, and re-layouts  3.54 us (7%)
  other arithmetic  1.27 us (3%)
    all_to_all x1, blocking collectives, local(): arrived = lax.all_to_all(payload, ('row', 'ctx'), 0, 0, tiled=True)  36.3 us
    pallas_call x1, Pallas kernels, local_attention(): pl.pallas_call(functools.partial(attention_kernel, shape), grid_spec=grid...  8.93 us
    reshape x1, local copies, waits for them, and re-layouts, local(): part_low = part.reshape(shards, head_share, per_owner, owners, HEAD_DIM)  1.47 us

profile of v5, /device:TPU:0, one launch (start us, length us, event | category | flops | bytes accessed | tf_op | source)
XLA Modules:
  0.0 50.1 jit_solution(15020104195938912603)
XLA Ops:
  0.0 8.9 %shard_map.55 = (bf16[16,256,128]{2,1,0:T(8,128)(2,1)}, f32[4,8,256]{2,1,0:T(8,128)}) custom-call(s32[2,8]{1,0:T(2,128)} %list_ref.1, s32[2]{0:T(128)} %count_ref.1, s32[1]{0:T(128)} %bitcast.first_ref, bf16[256,2048]{1,0:T(8,128)(2,1)} %q_ref.1, bf16[384,2048]{1,0:T(8,128)(2,1)} %k_ref.1, bf16[384,2048]{1,0:T(8,128)(2,1)} %v_ref.1), custom_call_target="tpu_custom_call" | custom-call | flops 805306368 | bytes 5242880 | tf_op jit(solution)/shard_map/pallas_call | solution.py:86
  8.9 0.0 copy-start
  8.9 1.5 %copy.12 = bf16[4,4,32,8,128]{4,2,1,0,3:T(8,128)(2,1)S(1)} copy(bf16[4,4,32,8,128]{4,3,2,1,0:T(8,128)(2,1)} %bitcast.39) | data formatting | bytes 2097152 | tf_op jit(solution)/shard_map/reshape | solution.py:128
  10.4 0.0 copy-done
  10.4 0.3 reshape.88
  10.7 0.2 copy.13
  11.0 0.1 copy.18
  11.2 0.1 reshape.92
  11.3 0.1 pad_maximum_fusion
  11.4 36.3 %all_to_all.5 = bf16[32,134,128]{2,1,0:T(8,128)(2,1)S(1)} all-to-all(bf16[32,134,128]{2,1,0:T(8,128)(2,1)S(1)} %pad_maximum_fusion), channel_id=1, replica_groups=mesh['ctx'=4,'row'=8] {'row','ctx'}, dimensions={0} | all-to-all | bytes 2195456 | tf_op jit(solution)/shard_map/all_to_all | solution.py:141
  47.7 0.2 reshape.91
  48.1 0.1 sub.44
  48.2 0.1 squeeze.11
  48.3 0.7 %multiply_reduce_fusion = f32[8,128,128]{2,1,0:T(8,128)S(1)} fusion(bf16[8,4,134,128]{3,2,1,0:T(8,128)(2,1)S(1)} %bitcast.35, f32[8,4,128]{2,1,0:T(4,128)S(1)} %subtract_exponential_fusion), kind=kLoop, calls=%fused_computation | loop fusion | flops 1441792 | bytes 1589248 | tf_op jit(solution)/shard_map/reduce_sum | solution.py:153
  49.0 0.2 divide_convert_fusion
  49.3 0.1 copy.17
  49.4 0.7 %copy.24 = bf16[32,8,4,128]{3,1,2,0:T(8,128)(2,1)} copy(bf16[32,8,4,128]{3,2,1,0:T(4,128)(2,1)S(1)} %bitcast.40) | data formatting | bytes 524288
  (8 shorter events, 0.3 us)
Async XLA Ops:
  8.9 1.5 %copy-start = (f32[4,8,256]{2,1,0:T(8,128)S(1)}, f32[4,8,256]{2,1,0:T(8,128)}, u32[]{:S(2)}) copy-start(f32[4,8,256]{2,1,0:T(8,128)} %get-tuple-element.8) | copy-start | bytes 98308

commit v6 on v5

--- a/solution.py
+++ b/solution.py
@@ -16,8 +16,8 @@
 
 
 def attention_kernel(shape, list_ref, count_ref, first_ref, q_ref, k_ref, v_ref, part_ref, stat_ref,
-                     bias_ref, any_ref):
-    rows, head_share, q_blocks, k_blocks, max_sel = shape
+                     bias_ref, dead_ref, out_scr, stat_scr):
+    rows, owners, per_owner, head_share, q_blocks, k_blocks, max_sel = shape
 
     @pl.when(pl.program_id(0) == 0)
     def _():
@@ -30,41 +30,47 @@
                     found = (list_ref[a, slot] == first + b) & (slot < count_ref[a])
                     hit = jnp.maximum(hit, jnp.where(found, 1, 0).astype(jnp.int32))
                 any_live = jnp.maximum(any_live, hit)
-                bias = jnp.where(hit > 0, 0.0, masked_fill).astype(jnp.float32)
-                bias_ref[a * BLOCK : (a + 1) * BLOCK, b * BLOCK : (b + 1) * BLOCK] = jnp.full(
-                    (BLOCK, BLOCK), bias, jnp.float32
-                )
-            any_ref[a * BLOCK : (a + 1) * BLOCK, :] = jnp.full((BLOCK, HEAD_DIM), any_live, jnp.int32)
+                bias_ref[a * k_blocks + b] = jnp.where(hit > 0, 0.0, masked_fill).astype(jnp.float32)
+            dead_ref[a] = jnp.where(any_live > 0, 0.0, jnp.inf).astype(jnp.float32)
+        stat_scr[...] = jnp.zeros_like(stat_scr)
 
     score_scale = 1.0 / HEAD_DIM**0.5
-    row_live = any_ref[:, 0:1] > 0
-    lane = lax.broadcasted_iota(jnp.int32, (rows, HEAD_DIM), 1)
-    stats = jnp.zeros((rows, HEAD_DIM), jnp.float32)
     for hl in range(head_share):
         cols = slice(hl * HEAD_DIM, (hl + 1) * HEAD_DIM)
-        scores = lax.dot_general(
-            q_ref[:, cols], k_ref[:, cols], (((1,), (1,)), ((), ())), preferred_element_type=jnp.float32
-        )
-        scores = scores * score_scale + bias_ref[...]
-        seg_max = jnp.max(scores, axis=1, keepdims=True)
-        probs = jnp.exp(scores - seg_max)
-        seg_total = jnp.where(row_live, jnp.sum(probs, axis=1, keepdims=True), 0.0)
-        seg_out = jnp.dot(probs.astype(jnp.bfloat16), v_ref[:, cols], preferred_element_type=jnp.float32)
-        part_ref[hl] = jnp.where(row_live, seg_out, 0.0).astype(jnp.bfloat16)
-        stats = jnp.where(lane == hl, seg_max, stats)
-        stats = jnp.where(lane == head_share + hl, seg_total, stats)
-    stat_ref[0] = jnp.transpose(stats)[: 2 * head_share]
+        for a in range(q_blocks):
+            here = slice(a * BLOCK, (a + 1) * BLOCK)
+            scores = lax.dot_general(
+                q_ref[here, cols], k_ref[:, cols], (((1,), (1,)), ((), ())), preferred_element_type=jnp.float32
+            )
+            bias = jnp.concatenate(
+                [jnp.full((1, BLOCK), bias_ref[a * k_blocks + b], jnp.float32) for b in range(k_blocks)], axis=1
+            )
+            scores = scores * score_scale + bias
+            seg_max = jnp.max(scores, axis=1, keepdims=True)
+            probs = jnp.exp(scores - (seg_max + dead_ref[a]))
+            seg_total = jnp.sum(probs, axis=1, keepdims=True)
+            out_scr[here, :] = jnp.dot(
+                probs.astype(jnp.bfloat16), v_ref[:, cols], preferred_element_type=jnp.float32
+            )
+            stat_scr[here, hl : hl + 1] = seg_max
+            stat_scr[here, head_share + hl : head_share + hl + 1] = seg_total
+        for r in range(owners):
+            part_ref[r, hl * per_owner : (hl + 1) * per_owner, :] = out_scr[
+                pl.ds(r, per_owner, stride=owners), :
+            ].astype(jnp.bfloat16)
+    stat_ref[0] = jnp.transpose(stat_scr[...])[: 2 * head_share]
 
 
-def local_attention(queries, keys, values, block_list, block_count, first_block, shards):
+def local_attention(queries, keys, values, block_list, block_count, first_block, owners, shards, dest_rows):
     rows = queries.shape[0]
     ctx_span = keys.shape[0]
+    per_owner = rows // owners
     head_share = HEADS // shards
     share_width = head_share * HEAD_DIM
     q_blocks = rows // BLOCK
     k_blocks = ctx_span // BLOCK
     max_sel = block_list.shape[1]
-    shape = (rows, head_share, q_blocks, k_blocks, max_sel)
+    shape = (rows, owners, per_owner, head_share, q_blocks, k_blocks, max_sel)
     grid_spec = pltpu.PrefetchScalarGridSpec(
         num_scalar_prefetch=3,
         grid=(shards,),
@@ -74,12 +80,14 @@
             pl.BlockSpec((ctx_span, share_width), lambda g, *_: (0, g)),
         ],
         out_specs=[
-            pl.BlockSpec((head_share, rows, HEAD_DIM), lambda g, *_: (g, 0, 0)),
+            pl.BlockSpec((owners, None, head_share * per_owner, HEAD_DIM), lambda g, *_: (0, g, 0, 0)),
             pl.BlockSpec((1, 2 * head_share, rows), lambda g, *_: (g, 0, 0)),
         ],
         scratch_shapes=[
-            pltpu.VMEM((rows, ctx_span), jnp.float32),
-            pltpu.VMEM((rows, HEAD_DIM), jnp.int32),
+            pltpu.SMEM((q_blocks * k_blocks,), jnp.float32),
+            pltpu.SMEM((q_blocks,), jnp.float32),
+            pltpu.VMEM((rows, HEAD_DIM), jnp.float32),
+            pltpu.VMEM((rows, HEAD_DIM), jnp.float32),
         ],
     )
     flops = 4 * HEADS * rows * ctx_span * HEAD_DIM
@@ -87,7 +95,7 @@
         functools.partial(attention_kernel, shape),
         grid_spec=grid_spec,
         out_shape=[
-            jax.ShapeDtypeStruct((HEADS, rows, HEAD_DIM), jnp.bfloat16),
+            jax.ShapeDtypeStruct((owners, shards, dest_rows, HEAD_DIM), jnp.bfloat16),
             jax.ShapeDtypeStruct((shards, 2 * head_share, rows), jnp.float32),
         ],
         compiler_params=pltpu.CompilerParams(dimension_semantics=("arbitrary",)),
@@ -122,21 +130,22 @@
     share_width = head_share * HEAD_DIM
     blocks_here = ctx_span // BLOCK
     first_block = (lax.axis_index("ctx") * blocks_here).astype(jnp.int32).reshape(1)
+    stat_count = 3 * 2 * head_share * per_owner
+    stat_rows = -(-stat_count // HEAD_DIM)
+    part_rows = head_share * per_owner
     part, stat = local_attention(
-        queries, keys, values, block_list.astype(jnp.int32), block_count.astype(jnp.int32), first_block, shards
-    )
-    part_low = part.reshape(shards, head_share, per_owner, owners, HEAD_DIM)
-    part_low = jnp.transpose(part_low, (3, 0, 1, 2, 4)).reshape(
-        owners * shards, head_share * per_owner, HEAD_DIM
+        queries, keys, values, block_list.astype(jnp.int32), block_count.astype(jnp.int32), first_block,
+        owners, shards, part_rows + stat_rows,
     )
     stats = jnp.transpose(stat.reshape(shards, 2, head_share, per_owner, owners), (4, 0, 1, 2, 3))
     stats = stats.reshape(owners * shards, 2, head_share, per_owner)
-    stat_count = 3 * 2 * head_share * per_owner
-    stat_rows = -(-stat_count // HEAD_DIM)
     stat_low = split_three(stats).reshape(owners * shards, stat_count)
     stat_low = jnp.pad(stat_low, ((0, 0), (0, stat_rows * HEAD_DIM - stat_count)))
-    payload = jnp.concatenate(
-        [part_low, stat_low.reshape(owners * shards, stat_rows, HEAD_DIM)], axis=1
+    payload = lax.dynamic_update_slice_in_dim(
+        part.reshape(owners * shards, part_rows + stat_rows, HEAD_DIM),
+        stat_low.reshape(owners * shards, stat_rows, HEAD_DIM),
+        part_rows,
+        axis=1,
     )
     arrived = lax.all_to_all(payload, ("row", "ctx"), 0, 0, tiled=True)
     arrived = arrived.reshape(owners, shards, head_share * per_owner + stat_rows, HEAD_DIM)

time: 50.3 us -> 54.8 us (1.089)
  Pallas kernels: 8.93 us -> 11.8 us
  other arithmetic: 1.27 us -> 2.3 us
    pallas_call x1, Pallas kernels: 8.93 us -> 11.8 us  [local_attention(): pl.pallas_call(functools.partial(attention_kernel, shape), grid_spec=grid...]
    reshape x1 -> x0, local copies, waits for them, and re-layouts: 1.47 us -> none  [local(): part_low = part.reshape(shards, head_share, per_owner, owners, HEAD_DIM)]
    reduce_sum x1, other arithmetic: 0.73 us -> 1.86 us  [local(): numerator = jnp.sum(part_in.astype(jnp.float32) * weight[..., None], axis=1)]
    reshape x1, local copies, waits for them, and re-layouts: 0.31 us -> 1.06 us  [local(): stat.reshape(shards, 2, head_share, per_owner, owners)]
    unnamed x4 -> x3, local copies, waits for them, and re-layouts: 0.77 us -> 1.42 us
where the time goes in v6:
time: 54.8 us; the launch traced here: 54.6 us
  blocking collectives  36.3 us (66%)
  Pallas kernels  11.8 us (22%)
  local copies, waits for them, and re-layouts  4.02 us (7%)
  other arithmetic  2.3 us (4%)
    all_to_all x1, blocking collectives, local(): arrived = lax.all_to_all(payload, ('row', 'ctx'), 0, 0, tiled=True)  36.3 us
    pallas_call x1, Pallas kernels, local_attention(): pl.pallas_call(functools.partial(attention_kernel, shape), grid_spec=grid...  11.8 us
    reduce_sum x1, other arithmetic, local(): numerator = jnp.sum(part_in.astype(jnp.float32) * weight[..., None], axis=1)  1.86 us
    unnamed x3, local copies, waits for them, and re-layouts  1.42 us

profile of v6, /device:TPU:0, one launch (start us, length us, event | category | flops | bytes accessed | tf_op | source)
XLA Modules:
  0.0 54.6 jit_solution(9081386375863987592)
XLA Ops:
  0.0 11.8 %shard_map.55 = (bf16[8,4,134,128]{3,2,1,0:T(8,128)(2,1)}, f32[4,8,256]{2,1,0:T(8,128)}) custom-call(s32[2,8]{1,0:T(2,128)} %list_ref.1, s32[2]{0:T(128)} %count_ref.1, s32[1]{0:T(128)} %bitcast.first_ref, bf16[256,2048]{1,0:T(8,128)(2,1)} %q_ref.1, bf16[384,2048]{1,0:T(8,128)(2,1)} %k_ref.1, bf16[384,2048]{1,0:T(8,128)(2,1)} %v_ref.1), custom_call_target="tpu_custom_call" | custom-call | flops 805306368 | bytes 5242880 | tf_op jit(solution)/shard_map/pallas_call | solution.py:94
  11.8 1.1 %reshape.84 = f32[4,2,4,32,8]{4,3,2,1,0:T(8,128)S(1)} reshape(f32[4,8,256]{2,1,0:T(8,128)} %get-tuple-element.8) | data formatting | bytes 65536 | tf_op jit(solution)/shard_map/reshape | solution.py:140
  12.9 0.0 copy-start
  12.9 0.2 copy.28
  13.2 0.1 copy.37
  13.3 0.1 reshape.88
  13.5 0.7 %copy-done = bf16[8,4,134,128]{3,2,1,0:T(8,128)(2,1)S(1)} copy-done((bf16[8,4,134,128]{3,2,1,0:T(8,128)(2,1)S(1)}, bf16[8,4,134,128]{3,2,1,0:T(8,128)(2,1)}, u32[]{:S(2)}) %copy-start) | copy-done | bytes 1097752
  14.2 36.3 %all_to_all.5 = bf16[32,134,128]{2,1,0:T(8,128)(2,1)S(1)} all-to-all(bf16[32,134,128]{2,1,0:T(8,128)(2,1)S(1)} %constant_dynamic-update-slice_fusion), channel_id=1, replica_groups=mesh['ctx'=4,'row'=8] {'row','ctx'}, dimensions={0} | all-to-all | bytes 2195456 | tf_op jit(solution)/shard_map/all_to_all | solution.py:150
  50.4 0.2 copy.31
  50.6 0.2 reshape.87
  51.0 0.1 reshape.89
  51.1 0.1 sub.44
  51.2 0.3 copy.33
  51.5 1.9 %multiply_reduce_fusion = f32[8,128,128]{2,0,1:T(8,128)S(1)} fusion(bf16[8,4,134,128]{3,1,0,2:T(4,128)(2,1)S(1)} %bitcast.32, f32[8,4,128]{1,0,2:T(8,128)S(1)} %copy.33), kind=kLoop, calls=%fused_computation | loop fusion | flops 1441792 | bytes 1589248 | tf_op jit(solution)/shard_map/reduce_sum | solution.py:162
  53.3 0.1 copy.34
  53.5 0.2 divide_convert_fusion
  53.7 0.1 copy.36
  53.8 0.7 %copy.52 = bf16[32,8,4,128]{3,1,2,0:T(8,128)(2,1)} copy(bf16[32,8,4,128]{3,2,1,0:T(4,128)(2,1)S(1)} %bitcast.36) | data formatting | bytes 524288
  (8 shorter events, 0.3 us)
Async XLA Ops:
  12.9 1.3 %copy-start = (bf16[8,4,134,128]{3,2,1,0:T(8,128)(2,1)S(1)}, bf16[8,4,134,128]{3,2,1,0:T(8,128)(2,1)}, u32[]{:S(2)}) copy-start(bf16[8,4,134,128]{3,2,1,0:T(8,128)(2,1)} %get-tuple-element.7) | copy-start | bytes 3293188

commit v7 on v5

--- a/solution.py
+++ b/solution.py
@@ -34,10 +34,11 @@
                 bias_ref[a * BLOCK : (a + 1) * BLOCK, b * BLOCK : (b + 1) * BLOCK] = jnp.full(
                     (BLOCK, BLOCK), bias, jnp.float32
                 )
-            any_ref[a * BLOCK : (a + 1) * BLOCK, :] = jnp.full((BLOCK, HEAD_DIM), any_live, jnp.int32)
+            dead = jnp.where(any_live > 0, 0.0, jnp.inf).astype(jnp.float32)
+            any_ref[a * BLOCK : (a + 1) * BLOCK, :] = jnp.full((BLOCK, HEAD_DIM), dead, jnp.float32)
 
     score_scale = 1.0 / HEAD_DIM**0.5
-    row_live = any_ref[:, 0:1] > 0
+    dead_row = any_ref[:, 0:1]
     lane = lax.broadcasted_iota(jnp.int32, (rows, HEAD_DIM), 1)
     stats = jnp.zeros((rows, HEAD_DIM), jnp.float32)
     for hl in range(head_share):
@@ -47,10 +48,10 @@
         )
         scores = scores * score_scale + bias_ref[...]
         seg_max = jnp.max(scores, axis=1, keepdims=True)
-        probs = jnp.exp(scores - seg_max)
-        seg_total = jnp.where(row_live, jnp.sum(probs, axis=1, keepdims=True), 0.0)
+        probs = jnp.exp(scores - (seg_max + dead_row))
+        seg_total = jnp.sum(probs, axis=1, keepdims=True)
         seg_out = jnp.dot(probs.astype(jnp.bfloat16), v_ref[:, cols], preferred_element_type=jnp.float32)
-        part_ref[hl] = jnp.where(row_live, seg_out, 0.0).astype(jnp.bfloat16)
+        part_ref[hl] = seg_out.astype(jnp.bfloat16)
         stats = jnp.where(lane == hl, seg_max, stats)
         stats = jnp.where(lane == head_share + hl, seg_total, stats)
     stat_ref[0] = jnp.transpose(stats)[: 2 * head_share]
@@ -79,7 +80,7 @@
         ],
         scratch_shapes=[
             pltpu.VMEM((rows, ctx_span), jnp.float32),
-            pltpu.VMEM((rows, HEAD_DIM), jnp.int32),
+            pltpu.VMEM((rows, HEAD_DIM), jnp.float32),
         ],
     )
     flops = 4 * HEADS * rows * ctx_span * HEAD_DIM
@@ -126,7 +127,7 @@
         queries, keys, values, block_list.astype(jnp.int32), block_count.astype(jnp.int32), first_block, shards
     )
     part_low = part.reshape(shards, head_share, per_owner, owners, HEAD_DIM)
-    part_low = jnp.transpose(part_low, (3, 0, 1, 2, 4)).reshape(
+    part_low = jnp.transpose(part_low, (3, 0, 2, 1, 4)).reshape(
         owners * shards, head_share * per_owner, HEAD_DIM
     )
     stats = jnp.transpose(stat.reshape(shards, 2, head_share, per_owner, owners), (4, 0, 1, 2, 3))
@@ -140,7 +141,7 @@
     )
     arrived = lax.all_to_all(payload, ("row", "ctx"), 0, 0, tiled=True)
     arrived = arrived.reshape(owners, shards, head_share * per_owner + stat_rows, HEAD_DIM)
-    part_in = arrived[:, :, : head_share * per_owner].reshape(owners, shards, head_share, per_owner, HEAD_DIM)
+    part_in = arrived[:, :, : head_share * per_owner].reshape(owners, shards, per_owner, head_share, HEAD_DIM)
     stat_in = arrived[:, :, head_share * per_owner :].reshape(owners * shards, stat_rows * HEAD_DIM)
     stats_in = join_three(
         stat_in[:, :stat_count].reshape(owners * shards, 3, 2, head_share, per_owner)
@@ -150,9 +151,11 @@
     row_best = jnp.max(maxima, axis=1)
     weight = jnp.exp(maxima - row_best[:, None])
     total_sum = jnp.sum(totals * weight, axis=1)
+    weight = jnp.swapaxes(weight, 2, 3)
+    total_sum = jnp.swapaxes(total_sum, 1, 2)
     numerator = jnp.sum(part_in.astype(jnp.float32) * weight[..., None], axis=1)
     attended = numerator / total_sum[..., None]
-    attended_low = jnp.transpose(attended, (0, 2, 1, 3)).reshape(row_count, share_width)
+    attended_low = attended.reshape(row_count, share_width)
     return attended_low.astype(jnp.bfloat16)
 
 

time: 50.3 us -> 52.8 us (1.050)
  Pallas kernels: 8.93 us -> 10.1 us
  local copies, waits for them, and re-layouts: 3.54 us -> 4.26 us
  other arithmetic: 1.27 us -> 1.94 us
    pallas_call x1, Pallas kernels: 8.93 us -> 10.1 us  [local_attention(): pl.pallas_call(functools.partial(attention_kernel, shape), grid_spec=grid...]
    convert_element_type x1, other arithmetic: 0.21 us -> 0.79 us  [local(): return attended_low.astype(jnp.bfloat16)]
    reshape x1, local copies, waits for them, and re-layouts: 1.47 us -> 2.04 us  [local(): part_low = part.reshape(shards, head_share, per_owner, owners, HEAD_DIM)]
where the time goes in v7:
time: 52.8 us; the launch traced here: 52.7 us
  blocking collectives  36.3 us (69%)
  Pallas kernels  10.1 us (19%)
  local copies, waits for them, and re-layouts  4.26 us (8%)
  other arithmetic  1.94 us (4%)
    all_to_all x1, blocking collectives, local(): arrived = lax.all_to_all(payload, ('row', 'ctx'), 0, 0, tiled=True)  36.3 us
    pallas_call x1, Pallas kernels, local_attention(): pl.pallas_call(functools.partial(attention_kernel, shape), grid_spec=grid...  10.1 us
    reshape x1, local copies, waits for them, and re-layouts, local(): part_low = part.reshape(shards, head_share, per_owner, owners, HEAD_DIM)  2.04 us

profile of v7, /device:TPU:0, one launch (start us, length us, event | category | flops | bytes accessed | tf_op | source)
XLA Modules:
  0.0 52.7 jit_solution(10281163299953829800)
XLA Ops:
  0.0 10.1 %shard_map.55 = (bf16[16,256,128]{2,1,0:T(8,128)(2,1)}, f32[4,8,256]{2,1,0:T(8,128)}) custom-call(s32[2,8]{1,0:T(2,128)} %list_ref.1, s32[2]{0:T(128)} %count_ref.1, s32[1]{0:T(128)} %bitcast.first_ref, bf16[256,2048]{1,0:T(8,128)(2,1)} %q_ref.1, bf16[384,2048]{1,0:T(8,128)(2,1)} %k_ref.1, bf16[384,2048]{1,0:T(8,128)(2,1)} %v_ref.1), custom_call_target="tpu_custom_call" | custom-call | flops 805306368 | bytes 5242880 | tf_op jit(solution)/shard_map/pallas_call | solution.py:87
  10.1 0.0 copy-start
  10.1 2.0 %copy.16 = bf16[4,4,32,8,128]{4,1,2,0,3:T(4,128)(2,1)S(1)} copy(bf16[4,4,32,8,128]{4,3,2,1,0:T(8,128)(2,1)} %bitcast.36) | data formatting | bytes 2097152 | tf_op jit(solution)/shard_map/reshape | solution.py:129
  12.1 0.0 copy-done
  12.1 0.3 reshape.84
  12.4 0.2 copy.17
  12.8 0.1 copy.25
  12.9 0.1 reshape.88
  13.0 0.1 pad_maximum_fusion
  13.1 36.3 %all_to_all.5 = bf16[32,134,128]{2,1,0:T(8,128)(2,1)S(1)} all-to-all(bf16[32,134,128]{2,1,0:T(8,128)(2,1)S(1)} %pad_maximum_fusion), channel_id=1, replica_groups=mesh['ctx'=4,'row'=8] {'row','ctx'}, dimensions={0} | all-to-all | bytes 2195456 | tf_op jit(solution)/shard_map/all_to_all | solution.py:142
  49.4 0.2 reshape.87
  49.8 0.1 copy.30
  49.8 0.2 copy.28
  50.0 0.2 copy.29
  50.2 0.1 fusion.1
  50.3 0.1 copy.22
  50.4 0.7 %multiply_reduce_fusion = f32[8,128,128]{2,1,0:T(8,128)S(1)} fusion(bf16[8,4,134,128]{3,2,1,0:T(8,128)(2,1)S(1)} %bitcast.31, f32[8,4,128]{2,1,0:T(4,128)S(1)} %copy.22), kind=kLoop, calls=%fused_computation | loop fusion | flops 1441792 | bytes 1589248 | tf_op jit(solution)/shard_map/reduce_sum | solution.py:156
  51.2 0.1 reduce_sum.21
  51.3 0.3 copy.24
  51.5 0.3 div.11
  51.9 0.8 %fusion = bf16[256,512]{1,0:T(8,128)(2,1)} fusion(f32[256,512]{1,0:T(8,128)S(1)} %reduce_sum.21, f32[32,8,4,128]{3,2,1,0:T(4,128)S(1)} %bitcast.33), kind=kLoop, calls=%fused_computation.3 | loop fusion | flops 262144 | bytes 1310720 | tf_op jit(solution)/shard_map/convert_element_type | solution.py:159
  (6 shorter events, 0.2 us)
Async XLA Ops:
  10.1 2.0 %copy-start = (f32[4,8,256]{2,1,0:T(8,128)S(1)}, f32[4,8,256]{2,1,0:T(8,128)}, u32[]{:S(2)}) copy-start(f32[4,8,256]{2,1,0:T(8,128)} %get-tuple-element.8) | copy-start | bytes 98308

commit v8 on v5

--- a/solution.py
+++ b/solution.py
@@ -16,7 +16,7 @@
 
 
 def attention_kernel(shape, list_ref, count_ref, first_ref, q_ref, k_ref, v_ref, part_ref, stat_ref,
-                     bias_ref, any_ref):
+                     bias_ref, dead_ref):
     rows, head_share, q_blocks, k_blocks, max_sel = shape
 
     @pl.when(pl.program_id(0) == 0)
@@ -31,29 +31,30 @@
                     hit = jnp.maximum(hit, jnp.where(found, 1, 0).astype(jnp.int32))
                 any_live = jnp.maximum(any_live, hit)
                 bias = jnp.where(hit > 0, 0.0, masked_fill).astype(jnp.float32)
-                bias_ref[a * BLOCK : (a + 1) * BLOCK, b * BLOCK : (b + 1) * BLOCK] = jnp.full(
+                bias_ref[b * BLOCK : (b + 1) * BLOCK, a * BLOCK : (a + 1) * BLOCK] = jnp.full(
                     (BLOCK, BLOCK), bias, jnp.float32
                 )
-            any_ref[a * BLOCK : (a + 1) * BLOCK, :] = jnp.full((BLOCK, HEAD_DIM), any_live, jnp.int32)
+            dead = jnp.where(any_live > 0, 0.0, jnp.inf).astype(jnp.float32)
+            dead_ref[:, a * BLOCK : (a + 1) * BLOCK] = jnp.full((8, BLOCK), dead, jnp.float32)
 
     score_scale = 1.0 / HEAD_DIM**0.5
-    row_live = any_ref[:, 0:1] > 0
-    lane = lax.broadcasted_iota(jnp.int32, (rows, HEAD_DIM), 1)
-    stats = jnp.zeros((rows, HEAD_DIM), jnp.float32)
+    dead_row = dead_ref[0:1, :]
     for hl in range(head_share):
         cols = slice(hl * HEAD_DIM, (hl + 1) * HEAD_DIM)
         scores = lax.dot_general(
-            q_ref[:, cols], k_ref[:, cols], (((1,), (1,)), ((), ())), preferred_element_type=jnp.float32
+            k_ref[:, cols], q_ref[:, cols], (((1,), (1,)), ((), ())), preferred_element_type=jnp.float32
         )
         scores = scores * score_scale + bias_ref[...]
-        seg_max = jnp.max(scores, axis=1, keepdims=True)
-        probs = jnp.exp(scores - seg_max)
-        seg_total = jnp.where(row_live, jnp.sum(probs, axis=1, keepdims=True), 0.0)
-        seg_out = jnp.dot(probs.astype(jnp.bfloat16), v_ref[:, cols], preferred_element_type=jnp.float32)
-        part_ref[hl] = jnp.where(row_live, seg_out, 0.0).astype(jnp.bfloat16)
-        stats = jnp.where(lane == hl, seg_max, stats)
-        stats = jnp.where(lane == head_share + hl, seg_total, stats)
-    stat_ref[0] = jnp.transpose(stats)[: 2 * head_share]
+        seg_max = jnp.max(scores, axis=0, keepdims=True)
+        probs = jnp.exp(scores - (seg_max + dead_row))
+        seg_total = jnp.sum(probs, axis=0, keepdims=True)
+        seg_out = lax.dot_general(
+            probs.astype(jnp.bfloat16), v_ref[:, cols], (((0,), (0,)), ((), ())),
+            preferred_element_type=jnp.float32,
+        )
+        part_ref[hl] = seg_out.astype(jnp.bfloat16)
+        stat_ref[0, hl : hl + 1, :] = seg_max
+        stat_ref[0, head_share + hl : head_share + hl + 1, :] = seg_total
 
 
 def local_attention(queries, keys, values, block_list, block_count, first_block, shards):
@@ -78,8 +79,8 @@
             pl.BlockSpec((1, 2 * head_share, rows), lambda g, *_: (g, 0, 0)),
         ],
         scratch_shapes=[
-            pltpu.VMEM((rows, ctx_span), jnp.float32),
-            pltpu.VMEM((rows, HEAD_DIM), jnp.int32),
+            pltpu.VMEM((ctx_span, rows), jnp.float32),
+            pltpu.VMEM((8, rows), jnp.float32),
         ],
     )
     flops = 4 * HEADS * rows * ctx_span * HEAD_DIM

time: 50.3 us -> 49.2 us (0.978)
  Pallas kernels: 8.93 us -> 7.71 us
    pallas_call x1, Pallas kernels: 8.93 us -> 7.71 us  [local_attention(): pl.pallas_call(functools.partial(attention_kernel, shape), grid_spec=grid...]
where the time goes in v8:
time: 49.2 us; the launch traced here: 48.9 us
  blocking collectives  36.3 us (74%)
  Pallas kernels  7.71 us (16%)
  local copies, waits for them, and re-layouts  3.54 us (7%)
  other arithmetic  1.27 us (3%)
    all_to_all x1, blocking collectives, local(): arrived = lax.all_to_all(payload, ('row', 'ctx'), 0, 0, tiled=True)  36.3 us
    pallas_call x1, Pallas kernels, local_attention(): pl.pallas_call(functools.partial(attention_kernel, shape), grid_spec=grid...  7.71 us
    reshape x1, local copies, waits for them, and re-layouts, local(): part_low = part.reshape(shards, head_share, per_owner, owners, HEAD_DIM)  1.47 us

profile of v8, /device:TPU:0, one launch (start us, length us, event | category | flops | bytes accessed | tf_op | source)
XLA Modules:
  0.0 48.9 jit_solution(16765424387320033249)
XLA Ops:
  0.0 7.7 %shard_map.55 = (bf16[16,256,128]{2,1,0:T(8,128)(2,1)}, f32[4,8,256]{2,1,0:T(8,128)}) custom-call(s32[2,8]{1,0:T(2,128)} %list_ref.1, s32[2]{0:T(128)} %count_ref.1, s32[1]{0:T(128)} %bitcast.first_ref, bf16[256,2048]{1,0:T(8,128)(2,1)} %q_ref.1, bf16[384,2048]{1,0:T(8,128)(2,1)} %k_ref.1, bf16[384,2048]{1,0:T(8,128)(2,1)} %v_ref.1), custom_call_target="tpu_custom_call" | custom-call | flops 805306368 | bytes 5242880 | tf_op jit(solution)/shard_map/pallas_call | solution.py:87
  7.7 0.0 copy-start
  7.7 1.5 %copy.12 = bf16[4,4,32,8,128]{4,2,1,0,3:T(8,128)(2,1)S(1)} copy(bf16[4,4,32,8,128]{4,3,2,1,0:T(8,128)(2,1)} %bitcast.39) | data formatting | bytes 2097152 | tf_op jit(solution)/shard_map/reshape | solution.py:129
  9.2 0.0 copy-done
  9.2 0.3 reshape.88
  9.5 0.2 copy.13
  9.8 0.1 copy.18
  9.9 0.1 reshape.92
  10.1 0.1 pad_maximum_fusion
  10.2 36.3 %all_to_all.5 = bf16[32,134,128]{2,1,0:T(8,128)(2,1)S(1)} all-to-all(bf16[32,134,128]{2,1,0:T(8,128)(2,1)S(1)} %pad_maximum_fusion), channel_id=1, replica_groups=mesh['ctx'=4,'row'=8] {'row','ctx'}, dimensions={0} | all-to-all | bytes 2195456 | tf_op jit(solution)/shard_map/all_to_all | solution.py:142
  46.5 0.2 reshape.91
  46.9 0.1 sub.44
  47.0 0.1 squeeze.11
  47.1 0.7 %multiply_reduce_fusion = f32[8,128,128]{2,1,0:T(8,128)S(1)} fusion(bf16[8,4,134,128]{3,2,1,0:T(8,128)(2,1)S(1)} %bitcast.35, f32[8,4,128]{2,1,0:T(4,128)S(1)} %subtract_exponential_fusion), kind=kLoop, calls=%fused_computation | loop fusion | flops 1441792 | bytes 1589248 | tf_op jit(solution)/shard_map/reduce_sum | solution.py:154
  47.8 0.2 divide_convert_fusion
  48.0 0.1 copy.17
  48.2 0.7 %copy.24 = bf16[32,8,4,128]{3,1,2,0:T(8,128)(2,1)} copy(bf16[32,8,4,128]{3,2,1,0:T(4,128)(2,1)S(1)} %bitcast.40) | data formatting | bytes 524288
  (8 shorter events, 0.3 us)
Async XLA Ops:
  7.7 1.5 %copy-start = (f32[4,8,256]{2,1,0:T(8,128)S(1)}, f32[4,8,256]{2,1,0:T(8,128)}, u32[]{:S(2)}) copy-start(f32[4,8,256]{2,1,0:T(8,128)} %get-tuple-element.8) | copy-start | bytes 98308

commit v9 on v8

--- a/solution.py
+++ b/solution.py
@@ -16,8 +16,8 @@
 
 
 def attention_kernel(shape, list_ref, count_ref, first_ref, q_ref, k_ref, v_ref, part_ref, stat_ref,
-                     bias_ref, dead_ref):
-    rows, head_share, q_blocks, k_blocks, max_sel = shape
+                     bias_ref, dead_ref, perm_ref):
+    rows, owners, per_owner, head_share, q_blocks, k_blocks, max_sel = shape
 
     @pl.when(pl.program_id(0) == 0)
     def _():
@@ -36,6 +36,11 @@
                 )
             dead = jnp.where(any_live > 0, 0.0, jnp.inf).astype(jnp.float32)
             dead_ref[:, a * BLOCK : (a + 1) * BLOCK] = jnp.full((8, BLOCK), dead, jnp.float32)
+        pos = lax.broadcasted_iota(jnp.int32, (rows, rows), 0)
+        frame = lax.broadcasted_iota(jnp.int32, (rows, rows), 1)
+        perm_ref[...] = jnp.where(
+            frame == (pos % per_owner) * owners + pos // per_owner, 1.0, 0.0
+        ).astype(jnp.bfloat16)
 
     score_scale = 1.0 / HEAD_DIM**0.5
     dead_row = dead_ref[0:1, :]
@@ -52,20 +57,22 @@
             probs.astype(jnp.bfloat16), v_ref[:, cols], (((0,), (0,)), ((), ())),
             preferred_element_type=jnp.float32,
         )
-        part_ref[hl] = seg_out.astype(jnp.bfloat16)
+        seg_out = jnp.dot(perm_ref[...], seg_out.astype(jnp.bfloat16), preferred_element_type=jnp.float32)
+        part_ref[:, hl] = seg_out.reshape(owners, per_owner, HEAD_DIM).astype(jnp.bfloat16)
         stat_ref[0, hl : hl + 1, :] = seg_max
         stat_ref[0, head_share + hl : head_share + hl + 1, :] = seg_total
 
 
-def local_attention(queries, keys, values, block_list, block_count, first_block, shards):
+def local_attention(queries, keys, values, block_list, block_count, first_block, owners, shards):
     rows = queries.shape[0]
+    per_owner = rows // owners
     ctx_span = keys.shape[0]
     head_share = HEADS // shards
     share_width = head_share * HEAD_DIM
     q_blocks = rows // BLOCK
     k_blocks = ctx_span // BLOCK
     max_sel = block_list.shape[1]
-    shape = (rows, head_share, q_blocks, k_blocks, max_sel)
+    shape = (rows, owners, per_owner, head_share, q_blocks, k_blocks, max_sel)
     grid_spec = pltpu.PrefetchScalarGridSpec(
         num_scalar_prefetch=3,
         grid=(shards,),
@@ -75,12 +82,13 @@
             pl.BlockSpec((ctx_span, share_width), lambda g, *_: (0, g)),
         ],
         out_specs=[
-            pl.BlockSpec((head_share, rows, HEAD_DIM), lambda g, *_: (g, 0, 0)),
+            pl.BlockSpec((owners, head_share, per_owner, HEAD_DIM), lambda g, *_: (0, g, 0, 0)),
             pl.BlockSpec((1, 2 * head_share, rows), lambda g, *_: (g, 0, 0)),
         ],
         scratch_shapes=[
             pltpu.VMEM((ctx_span, rows), jnp.float32),
             pltpu.VMEM((8, rows), jnp.float32),
+            pltpu.VMEM((rows, rows), jnp.bfloat16),
         ],
     )
     flops = 4 * HEADS * rows * ctx_span * HEAD_DIM
@@ -88,7 +96,7 @@
         functools.partial(attention_kernel, shape),
         grid_spec=grid_spec,
         out_shape=[
-            jax.ShapeDtypeStruct((HEADS, rows, HEAD_DIM), jnp.bfloat16),
+            jax.ShapeDtypeStruct((owners, HEADS, per_owner, HEAD_DIM), jnp.bfloat16),
             jax.ShapeDtypeStruct((shards, 2 * head_share, rows), jnp.float32),
         ],
         compiler_params=pltpu.CompilerParams(dimension_semantics=("arbitrary",)),
@@ -124,12 +132,9 @@
     blocks_here = ctx_span // BLOCK
     first_block = (lax.axis_index("ctx") * blocks_here).astype(jnp.int32).reshape(1)
     part, stat = local_attention(
-        queries, keys, values, block_list.astype(jnp.int32), block_count.astype(jnp.int32), first_block, shards
+        queries, keys, values, block_list.astype(jnp.int32), block_count.astype(jnp.int32), first_block, owners, shards
     )
-    part_low = part.reshape(shards, head_share, per_owner, owners, HEAD_DIM)
-    part_low = jnp.transpose(part_low, (3, 0, 1, 2, 4)).reshape(
-        owners * shards, head_share * per_owner, HEAD_DIM
-    )
+    part_low = part.reshape(owners * shards, head_share * per_owner, HEAD_DIM)
     stats = jnp.transpose(stat.reshape(shards, 2, head_share, per_owner, owners), (4, 0, 1, 2, 3))
     stats = stats.reshape(owners * shards, 2, head_share, per_owner)
     stat_count = 3 * 2 * head_share * per_owner

time: 49.2 us -> 51.7 us (1.051)
  Pallas kernels: 7.71 us -> 9.25 us
  other arithmetic: 1.27 us -> 2.39 us
    pallas_call x1, Pallas kernels: 7.71 us -> 9.25 us  [local_attention(): pl.pallas_call(functools.partial(attention_kernel, shape), grid_spec=grid...]
    reshape x1 -> x0, local copies, waits for them, and re-layouts: 1.47 us -> none  [local(): part_low = part.reshape(shards, head_share, per_owner, owners, HEAD_DIM)]
    reduce_sum x1, other arithmetic: 0.73 us -> 1.86 us  [local(): numerator = jnp.sum(part_in.astype(jnp.float32) * weight[..., None], axis=1)]
    reshape x1, local copies, waits for them, and re-layouts: 0.31 us -> 1.15 us  [local(): stat.reshape(shards, 2, head_share, per_owner, owners)]
where the time goes in v9:
time: 51.7 us; the launch traced here: 51.5 us
  blocking collectives  36.3 us (70%)
  Pallas kernels  9.25 us (18%)
  local copies, waits for them, and re-layouts  3.43 us (7%)
  other arithmetic  2.39 us (5%)
    all_to_all x1, blocking collectives, local(): arrived = lax.all_to_all(payload, ('row', 'ctx'), 0, 0, tiled=True)  36.3 us
    pallas_call x1, Pallas kernels, local_attention(): pl.pallas_call(functools.partial(attention_kernel, shape), grid_spec=grid...  9.25 us
    reduce_sum x1, other arithmetic, local(): numerator = jnp.sum(part_in.astype(jnp.float32) * weight[..., None], axis=1)  1.86 us
    reshape x1, local copies, waits for them, and re-layouts, local(): stat.reshape(shards, 2, head_share, per_owner, owners)  1.15 us

profile of v9, /device:TPU:0, one launch (start us, length us, event | category | flops | bytes accessed | tf_op | source)
XLA Modules:
  0.0 51.5 jit_solution(6162474461981376049)
XLA Ops:
  0.0 9.3 %shard_map.55 = (bf16[8,16,32,128]{3,2,1,0:T(8,128)(2,1)}, f32[4,8,256]{2,1,0:T(8,128)}) custom-call(s32[2,8]{1,0:T(2,128)} %list_ref.1, s32[2]{0:T(128)} %count_ref.1, s32[1]{0:T(128)} %bitcast.first_ref, bf16[256,2048]{1,0:T(8,128)(2,1)} %q_ref.1, bf16[384,2048]{1,0:T(8,128)(2,1)} %k_ref.1, bf16[384,2048]{1,0:T(8,128)(2,1)} %v_ref.1), custom_call_target="tpu_custom_call" | custom-call | flops 805306368 | bytes 5242880 | tf_op jit(solution)/shard_map/pallas_call | solution.py:95
  9.3 0.0 copy-start
  9.3 1.2 %reshape.84 = f32[4,2,4,32,8]{4,3,2,1,0:T(8,128)S(1)} reshape(f32[4,8,256]{2,1,0:T(8,128)} %get-tuple-element.8) | data formatting | bytes 65536 | tf_op jit(solution)/shard_map/reshape | solution.py:138
  10.4 0.2 copy.28
  10.7 0.1 copy.37
  10.8 0.1 reshape.88
  11.0 0.0 copy-done
  11.0 0.1 pad_maximum_fusion
  11.1 36.3 %all_to_all.5 = bf16[32,134,128]{2,1,0:T(8,128)(2,1)S(1)} all-to-all(bf16[32,134,128]{2,1,0:T(8,128)(2,1)S(1)} %pad_maximum_fusion), channel_id=1, replica_groups=mesh['ctx'=4,'row'=8] {'row','ctx'}, dimensions={0} | all-to-all | bytes 2195456 | tf_op jit(solution)/shard_map/all_to_all | solution.py:147
  47.4 0.2 copy.31
  47.6 0.2 reshape.87
  47.9 0.1 reshape.89
  48.0 0.1 sub.44
  48.1 0.3 copy.33
  48.4 1.9 %multiply_reduce_fusion = f32[8,128,128]{2,0,1:T(8,128)S(1)} fusion(bf16[8,4,134,128]{3,1,0,2:T(4,128)(2,1)S(1)} %bitcast.32, f32[8,4,128]{1,0,2:T(8,128)S(1)} %copy.33), kind=kLoop, calls=%fused_computation | loop fusion | flops 1441792 | bytes 1589248 | tf_op jit(solution)/shard_map/reduce_sum | solution.py:159
  50.3 0.1 copy.34
  50.4 0.2 divide_convert_fusion
  50.6 0.1 copy.36
  50.7 0.7 %copy.52 = bf16[32,8,4,128]{3,1,2,0:T(8,128)(2,1)} copy(bf16[32,8,4,128]{3,2,1,0:T(4,128)(2,1)S(1)} %bitcast.36) | data formatting | bytes 524288
  (7 shorter events, 0.2 us)
Async XLA Ops:
  9.3 1.7 %copy-start = (bf16[8,16,32,128]{3,2,1,0:T(8,128)(2,1)S(1)}, bf16[8,16,32,128]{3,2,1,0:T(8,128)(2,1)}, u32[]{:S(2)}) copy-start(bf16[8,16,32,128]{3,2,1,0:T(8,128)(2,1)} %get-tuple-element.7) | copy-start | bytes 3145732

commit v10 on v8

--- a/solution.py
+++ b/solution.py
@@ -100,6 +100,59 @@
     )(block_list, block_count, first_block, queries, keys, values)
 
 
+def combine_kernel(shape, arr_ref, out_ref):
+    owners, shards, per_owner, head_share, part_rows, stat_rows = shape
+    share = head_share * per_owner
+
+    def stat_column(stat_t, k):
+        base = k * share
+        if share % HEAD_DIM == 0:
+            return stat_t[:, base // HEAD_DIM : base // HEAD_DIM + 1]
+        return stat_t[base % HEAD_DIM : base % HEAD_DIM + share, base // HEAD_DIM : base // HEAD_DIM + 1]
+
+    def body(r, carry):
+        maxima, totals = [], []
+        for c in range(shards):
+            stat_t = jnp.transpose(arr_ref[r, c, part_rows:, :].astype(jnp.float32))
+            parts = [[stat_column(stat_t, part * 2 + kind) for kind in range(2)] for part in range(3)]
+            maxima.append((parts[0][0] + parts[1][0]) + parts[2][0])
+            totals.append((parts[0][1] + parts[1][1]) + parts[2][1])
+        best = maxima[0]
+        for c in range(1, shards):
+            best = jnp.maximum(best, maxima[c])
+        total = None
+        numer = None
+        for c in range(shards):
+            weight = jnp.exp(maxima[c] - best)
+            term = totals[c] * weight
+            total = term if total is None else total + term
+            piece = arr_ref[r, c, :part_rows, :].astype(jnp.float32) * weight
+            numer = piece if numer is None else numer + piece
+        attended = (numer / total).astype(jnp.bfloat16)
+        start = pl.multiple_of(r * per_owner, per_owner)
+        for hl in range(head_share):
+            out_ref[pl.ds(start, per_owner), hl * HEAD_DIM : (hl + 1) * HEAD_DIM] = attended[
+                hl * per_owner : (hl + 1) * per_owner
+            ]
+        return carry
+
+    lax.fori_loop(0, owners, body, 0)
+
+
+def combine(arrived, owners, shards, per_owner, head_share, part_rows, stat_rows):
+    shape = (owners, shards, per_owner, head_share, part_rows, stat_rows)
+    assert (head_share * per_owner) % HEAD_DIM == 0 or HEAD_DIM % (head_share * per_owner) == 0
+    return pl.pallas_call(
+        functools.partial(combine_kernel, shape),
+        in_specs=[pl.BlockSpec(memory_space=pltpu.VMEM)],
+        out_specs=pl.BlockSpec(memory_space=pltpu.VMEM),
+        out_shape=jax.ShapeDtypeStruct((owners * per_owner, head_share * HEAD_DIM), jnp.bfloat16),
+        cost_estimate=pl.CostEstimate(
+            flops=3 * arrived.size, transcendentals=owners * shards * 128, bytes_accessed=2 * arrived.size
+        ),
+    )(arrived.reshape(owners, shards, part_rows + stat_rows, HEAD_DIM))
+
+
 def split_three(x):
     hi = lax.reduce_precision(x, exponent_bits=8, mantissa_bits=7)
     rest = x - hi
@@ -140,21 +193,7 @@
         [part_low, stat_low.reshape(owners * shards, stat_rows, HEAD_DIM)], axis=1
     )
     arrived = lax.all_to_all(payload, ("row", "ctx"), 0, 0, tiled=True)
-    arrived = arrived.reshape(owners, shards, head_share * per_owner + stat_rows, HEAD_DIM)
-    part_in = arrived[:, :, : head_share * per_owner].reshape(owners, shards, head_share, per_owner, HEAD_DIM)
-    stat_in = arrived[:, :, head_share * per_owner :].reshape(owners * shards, stat_rows * HEAD_DIM)
-    stats_in = join_three(
-        stat_in[:, :stat_count].reshape(owners * shards, 3, 2, head_share, per_owner)
-    ).reshape(owners, shards, 2, head_share, per_owner)
-    maxima = stats_in[:, :, 0]
-    totals = stats_in[:, :, 1]
-    row_best = jnp.max(maxima, axis=1)
-    weight = jnp.exp(maxima - row_best[:, None])
-    total_sum = jnp.sum(totals * weight, axis=1)
-    numerator = jnp.sum(part_in.astype(jnp.float32) * weight[..., None], axis=1)
-    attended = numerator / total_sum[..., None]
-    attended_low = jnp.transpose(attended, (0, 2, 1, 3)).reshape(row_count, share_width)
-    return attended_low.astype(jnp.bfloat16)
+    return combine(arrived, owners, shards, per_owner, head_share, head_share * per_owner, stat_rows)
 
 
 def solution(mesh):

time: 49.2 us -> 53.4 us (1.085)
  Pallas kernels: 7.71 us -> 14.3 us
  local copies, waits for them, and re-layouts: 3.54 us -> 2.23 us
  other arithmetic: 1.27 us -> 0.18 us
    pallas_call x0 -> x1, Pallas kernels: none -> 6.61 us  [combine(): pl.pallas_call(functools.partial(combine_kernel, shape), in_specs=[pl.Blo...]
    reshape x1 -> x0, local copies, waits for them, and re-layouts: 1.47 us -> none  [local(): part_low = part.reshape(shards, head_share, per_owner, owners, HEAD_DIM)]
    transpose x0 -> x1, local copies, waits for them, and re-layouts: none -> 1.47 us  [local(): jnp.transpose(part_low, (3, 0, 1, 2, 4))]
    reduce_sum x2 -> x0, other arithmetic: 0.78 us -> none  [the longest x1 0.73 us: local(): numerator = jnp.sum(part_in.astype(jnp.float32) * weight[..., None], axis=1)]
    unnamed x4 -> x2, local copies, waits for them, and re-layouts: 0.77 us -> 0.01 us
where the time goes in v10:
time: 53.4 us; the launch traced here: 53.2 us
  blocking collectives  36.4 us (68%)
  Pallas kernels  14.3 us (27%)
  local copies, waits for them, and re-layouts  2.23 us (4%)
    all_to_all x1, blocking collectives, local(): arrived = lax.all_to_all(payload, ('row', 'ctx'), 0, 0, tiled=True)  36.4 us
    pallas_call x1, Pallas kernels, local_attention(): pl.pallas_call(functools.partial(attention_kernel, shape), grid_spec=grid...  7.7 us
    pallas_call x1, Pallas kernels, combine(): pl.pallas_call(functools.partial(combine_kernel, shape), in_specs=[pl.Blo...  6.61 us
    transpose x1, local copies, waits for them, and re-layouts, local(): jnp.transpose(part_low, (3, 0, 1, 2, 4))  1.47 us

profile of v10, /device:TPU:0, one launch (start us, length us, event | category | flops | bytes accessed | tf_op | source)
XLA Modules:
  0.0 53.2 jit_solution(4216876648814770078)
XLA Ops:
  0.0 7.7 %shard_map.55 = (bf16[16,256,128]{2,1,0:T(8,128)(2,1)}, f32[4,8,256]{2,1,0:T(8,128)}) custom-call(s32[2,8]{1,0:T(2,128)} %list_ref.1, s32[2]{0:T(128)} %count_ref.1, s32[1]{0:T(128)} %bitcast.first_ref, bf16[256,2048]{1,0:T(8,128)(2,1)} %q_ref.1, bf16[384,2048]{1,0:T(8,128)(2,1)} %k_ref.1, bf16[384,2048]{1,0:T(8,128)(2,1)} %v_ref.1), custom_call_target="tpu_custom_call" | custom-call | flops 805306368 | bytes 5242880 | tf_op jit(solution)/shard_map/pallas_call | solution.py:87
  7.7 0.0 copy-start
  7.7 1.5 %copy.7 = bf16[8,4,4,32,128]{4,3,2,1,0:T(8,128)(2,1)S(1)} copy(bf16[8,4,4,32,128]{4,0,3,2,1:T(8,128)(2,1)} %bitcast.11) | data formatting | bytes 2097152 | tf_op jit(solution)/shard_map/transpose | solution.py:183
  9.2 0.0 copy-done
  9.2 0.3 reshape.65
  9.5 0.2 copy.8
  9.8 0.1 copy.11
  9.9 0.1 reshape.68
  10.1 0.1 pad_maximum_fusion
  10.2 36.4 %all_to_all.5 = bf16[32,134,128]{2,1,0:T(8,128)(2,1)} all-to-all(bf16[32,134,128]{2,1,0:T(8,128)(2,1)S(1)} %pad_maximum_fusion), channel_id=1, replica_groups=mesh['ctx'=4,'row'=8] {'row','ctx'}, dimensions={0} | all-to-all | bytes 2195456 | tf_op jit(solution)/shard_map/all_to_all | solution.py:195
  46.5 6.6 %shard_map.56 = bf16[256,512]{1,0:T(8,128)(2,1)} custom-call(bf16[8,4,134,128]{3,2,1,0:T(8,128)(2,1)} %bitcast.8), custom_call_target="tpu_custom_call" | custom-call | flops 1646592 | bytes 1097728 | tf_op jit(solution)/shard_map/pallas_call | solution.py:145
  (2 shorter events, 0.1 us)
Async XLA Ops:
  7.7 1.5 %copy-start = (f32[4,8,256]{2,1,0:T(8,128)S(1)}, f32[4,8,256]{2,1,0:T(8,128)}, u32[]{:S(2)}) copy-start(f32[4,8,256]{2,1,0:T(8,128)} %get-tuple-element.8) | copy-start | bytes 98308

commit v11 on v8

--- a/solution.py
+++ b/solution.py
@@ -52,7 +52,7 @@
             probs.astype(jnp.bfloat16), v_ref[:, cols], (((0,), (0,)), ((), ())),
             preferred_element_type=jnp.float32,
         )
-        part_ref[hl] = seg_out.astype(jnp.bfloat16)
+        part_ref[hl] = seg_out
         stat_ref[0, hl : hl + 1, :] = seg_max
         stat_ref[0, head_share + hl : head_share + hl + 1, :] = seg_total
 
@@ -88,7 +88,7 @@
         functools.partial(attention_kernel, shape),
         grid_spec=grid_spec,
         out_shape=[
-            jax.ShapeDtypeStruct((HEADS, rows, HEAD_DIM), jnp.bfloat16),
+            jax.ShapeDtypeStruct((HEADS, rows, HEAD_DIM), jnp.float32),
             jax.ShapeDtypeStruct((shards, 2 * head_share, rows), jnp.float32),
         ],
         compiler_params=pltpu.CompilerParams(dimension_semantics=("arbitrary",)),
@@ -129,7 +129,7 @@
     part_low = part.reshape(shards, head_share, per_owner, owners, HEAD_DIM)
     part_low = jnp.transpose(part_low, (3, 0, 1, 2, 4)).reshape(
         owners * shards, head_share * per_owner, HEAD_DIM
-    )
+    ).astype(jnp.bfloat16)
     stats = jnp.transpose(stat.reshape(shards, 2, head_share, per_owner, owners), (4, 0, 1, 2, 3))
     stats = stats.reshape(owners * shards, 2, head_share, per_owner)
     stat_count = 3 * 2 * head_share * per_owner

time: 49.2 us -> 50.5 us (1.026)
  other arithmetic: 1.27 us -> 3.04 us
  local copies, waits for them, and re-layouts: 3.54 us -> 2.82 us
    convert_element_type x0 -> x1, other arithmetic: none -> 1.77 us  [local(): part_low = jnp.transpose(part_low, (3, 0, 1, 2, 4)).reshape(owners * shar...]
    reshape x1 -> x0, local copies, waits for them, and re-layouts: 1.47 us -> none  [local(): part_low = part.reshape(shards, head_share, per_owner, owners, HEAD_DIM)]
    unnamed x4, local copies, waits for them, and re-layouts: 0.77 us -> 1.28 us
where the time goes in v11:
time: 50.5 us; the launch traced here: 50.2 us
  blocking collectives  36.3 us (72%)
  Pallas kernels  7.93 us (16%)
  other arithmetic  3.04 us (6%)
  local copies, waits for them, and re-layouts  2.82 us (6%)
    all_to_all x1, blocking collectives, local(): arrived = lax.all_to_all(payload, ('row', 'ctx'), 0, 0, tiled=True)  36.3 us
    pallas_call x1, Pallas kernels, local_attention(): pl.pallas_call(functools.partial(attention_kernel, shape), grid_spec=grid...  7.93 us
    convert_element_type x1, other arithmetic, local(): part_low = jnp.transpose(part_low, (3, 0, 1, 2, 4)).reshape(owners * shar...  1.77 us
    unnamed x4, local copies, waits for them, and re-layouts  1.28 us

profile of v11, /device:TPU:0, one launch (start us, length us, event | category | flops | bytes accessed | tf_op | source)
XLA Modules:
  0.0 50.2 jit_solution(16302390512153179836)
XLA Ops:
  0.0 7.9 %shard_map.55 = (f32[16,256,128]{2,1,0:T(8,128)}, f32[4,8,256]{2,1,0:T(8,128)}) custom-call(s32[2,8]{1,0:T(2,128)} %list_ref.1, s32[2]{0:T(128)} %count_ref.1, s32[1]{0:T(128)} %bitcast.first_ref, bf16[256,2048]{1,0:T(8,128)(2,1)} %q_ref.1, bf16[384,2048]{1,0:T(8,128)(2,1)} %k_ref.1, bf16[384,2048]{1,0:T(8,128)(2,1)} %v_ref.1), custom_call_target="tpu_custom_call" | custom-call | flops 805306368 | bytes 5242880 | tf_op jit(solution)/shard_map/pallas_call | solution.py:87
  7.9 1.8 %convert_element_type.33 = bf16[16,256,128]{2,1,0:T(8,128)(2,1)S(1)} convert(f32[16,256,128]{2,1,0:T(8,128)} %get-tuple-element.7) | non-fusion elementwise | flops 524288 | bytes 3145728 | tf_op jit(solution)/shard_map/convert_element_type | solution.py:132
  9.7 0.0 copy-start
  9.7 0.2 copy.12
  10.0 0.5 %copy-done = f32[4,8,256]{2,1,0:T(8,128)S(1)} copy-done((f32[4,8,256]{2,1,0:T(8,128)S(1)}, f32[4,8,256]{2,1,0:T(8,128)}, u32[]{:S(2)}) %copy-start) | copy-done | bytes 32792
  10.5 0.3 reshape.84
  10.8 0.2 copy.13
  11.1 0.1 copy.18
  11.2 0.1 reshape.88
  11.4 0.1 pad_maximum_fusion
  11.4 36.3 %all_to_all.5 = bf16[32,134,128]{2,1,0:T(8,128)(2,1)S(1)} all-to-all(bf16[32,134,128]{2,1,0:T(8,128)(2,1)S(1)} %pad_maximum_fusion), channel_id=1, replica_groups=mesh['ctx'=4,'row'=8] {'row','ctx'}, dimensions={0} | all-to-all | bytes 2195456 | tf_op jit(solution)/shard_map/all_to_all | solution.py:142
  47.8 0.2 reshape.87
  48.1 0.1 sub.44
  48.2 0.1 squeeze.11
  48.3 0.7 %multiply_reduce_fusion = f32[8,128,128]{2,1,0:T(8,128)S(1)} fusion(bf16[8,4,134,128]{3,2,1,0:T(8,128)(2,1)S(1)} %bitcast.35, f32[8,4,128]{2,1,0:T(4,128)S(1)} %subtract_exponential_fusion), kind=kLoop, calls=%fused_computation | loop fusion | flops 1441792 | bytes 1589248 | tf_op jit(solution)/shard_map/reduce_sum | solution.py:154
  49.1 0.2 divide_convert_fusion
  49.3 0.1 copy.17
  49.4 0.7 %copy.24 = bf16[32,8,4,128]{3,1,2,0:T(8,128)(2,1)} copy(bf16[32,8,4,128]{3,2,1,0:T(4,128)(2,1)S(1)} %bitcast.40) | data formatting | bytes 524288
  (8 shorter events, 0.3 us)
Async XLA Ops:
  9.7 0.8 %copy-start = (f32[4,8,256]{2,1,0:T(8,128)S(1)}, f32[4,8,256]{2,1,0:T(8,128)}, u32[]{:S(2)}) copy-start(f32[4,8,256]{2,1,0:T(8,128)} %get-tuple-element.8) | copy-start | bytes 98308

commit v12 on v8

--- a/solution.py
+++ b/solution.py
@@ -10,6 +10,7 @@
 HEADS = 16
 HEAD_DIM = 128
 BLOCK = 128
+HEADS_PER_STEP = 8
 
 
 masked_fill = -1e30
@@ -54,29 +55,29 @@
         )
         part_ref[hl] = seg_out.astype(jnp.bfloat16)
         stat_ref[0, hl : hl + 1, :] = seg_max
-        stat_ref[0, head_share + hl : head_share + hl + 1, :] = seg_total
+        stat_ref[1, hl : hl + 1, :] = seg_total
 
 
 def local_attention(queries, keys, values, block_list, block_count, first_block, shards):
     rows = queries.shape[0]
     ctx_span = keys.shape[0]
-    head_share = HEADS // shards
-    share_width = head_share * HEAD_DIM
+    step_heads = HEADS_PER_STEP
+    step_width = step_heads * HEAD_DIM
     q_blocks = rows // BLOCK
     k_blocks = ctx_span // BLOCK
     max_sel = block_list.shape[1]
-    shape = (rows, head_share, q_blocks, k_blocks, max_sel)
+    shape = (rows, step_heads, q_blocks, k_blocks, max_sel)
     grid_spec = pltpu.PrefetchScalarGridSpec(
         num_scalar_prefetch=3,
-        grid=(shards,),
+        grid=(HEADS // step_heads,),
         in_specs=[
-            pl.BlockSpec((rows, share_width), lambda g, *_: (0, g)),
-            pl.BlockSpec((ctx_span, share_width), lambda g, *_: (0, g)),
-            pl.BlockSpec((ctx_span, share_width), lambda g, *_: (0, g)),
+            pl.BlockSpec((rows, step_width), lambda g, *_: (0, g)),
+            pl.BlockSpec((ctx_span, step_width), lambda g, *_: (0, g)),
+            pl.BlockSpec((ctx_span, step_width), lambda g, *_: (0, g)),
         ],
         out_specs=[
-            pl.BlockSpec((head_share, rows, HEAD_DIM), lambda g, *_: (g, 0, 0)),
-            pl.BlockSpec((1, 2 * head_share, rows), lambda g, *_: (g, 0, 0)),
+            pl.BlockSpec((step_heads, rows, HEAD_DIM), lambda g, *_: (g, 0, 0)),
+            pl.BlockSpec((2, step_heads, rows), lambda g, *_: (0, g, 0)),
         ],
         scratch_shapes=[
             pltpu.VMEM((ctx_span, rows), jnp.float32),
@@ -89,7 +90,7 @@
         grid_spec=grid_spec,
         out_shape=[
             jax.ShapeDtypeStruct((HEADS, rows, HEAD_DIM), jnp.bfloat16),
-            jax.ShapeDtypeStruct((shards, 2 * head_share, rows), jnp.float32),
+            jax.ShapeDtypeStruct((2, HEADS, rows), jnp.float32),
         ],
         compiler_params=pltpu.CompilerParams(dimension_semantics=("arbitrary",)),
         cost_estimate=pl.CostEstimate(
@@ -130,7 +131,7 @@
     part_low = jnp.transpose(part_low, (3, 0, 1, 2, 4)).reshape(
         owners * shards, head_share * per_owner, HEAD_DIM
     )
-    stats = jnp.transpose(stat.reshape(shards, 2, head_share, per_owner, owners), (4, 0, 1, 2, 3))
+    stats = jnp.transpose(stat.reshape(2, shards, head_share, per_owner, owners), (4, 1, 0, 2, 3))
     stats = stats.reshape(owners * shards, 2, head_share, per_owner)
     stat_count = 3 * 2 * head_share * per_owner
     stat_rows = -(-stat_count // HEAD_DIM)

time: 49.2 us -> 48.3 us (0.982)
  Pallas kernels: 7.71 us -> 6.94 us
    pallas_call x1, Pallas kernels: 7.71 us -> 6.94 us  [local_attention(): pl.pallas_call(functools.partial(attention_kernel, shape), grid_spec=grid...]
where the time goes in v12:
time: 48.3 us; the launch traced here: 48.1 us
  blocking collectives  36.3 us (75%)
  Pallas kernels  6.94 us (14%)
  local copies, waits for them, and re-layouts  3.54 us (7%)
  other arithmetic  1.27 us (3%)
    all_to_all x1, blocking collectives, local(): arrived = lax.all_to_all(payload, ('row', 'ctx'), 0, 0, tiled=True)  36.3 us
    pallas_call x1, Pallas kernels, local_attention(): pl.pallas_call(functools.partial(attention_kernel, shape), grid_spec=grid...  6.94 us
    reshape x1, local copies, waits for them, and re-layouts, local(): part_low = part.reshape(shards, head_share, per_owner, owners, HEAD_DIM)  1.47 us

profile of v12, /device:TPU:0, one launch (start us, length us, event | category | flops | bytes accessed | tf_op | source)
XLA Modules:
  0.0 48.1 jit_solution(17459301081139694774)
XLA Ops:
  0.0 6.9 %shard_map.55 = (bf16[16,256,128]{2,1,0:T(8,128)(2,1)}, f32[2,16,256]{2,1,0:T(8,128)}) custom-call(s32[2,8]{1,0:T(2,128)} %list_ref.1, s32[2]{0:T(128)} %count_ref.1, s32[1]{0:T(128)} %bitcast.first_ref, bf16[256,2048]{1,0:T(8,128)(2,1)} %q_ref.1, bf16[384,2048]{1,0:T(8,128)(2,1)} %k_ref.1, bf16[384,2048]{1,0:T(8,128)(2,1)} %v_ref.1), custom_call_target="tpu_custom_call" | custom-call | flops 805306368 | bytes 5242880 | tf_op jit(solution)/shard_map/pallas_call | solution.py:88
  6.9 0.0 copy-start
  6.9 1.5 %copy.12 = bf16[4,4,32,8,128]{4,2,1,0,3:T(8,128)(2,1)S(1)} copy(bf16[4,4,32,8,128]{4,3,2,1,0:T(8,128)(2,1)} %bitcast.39) | data formatting | bytes 2097152 | tf_op jit(solution)/shard_map/reshape | solution.py:130
  8.4 0.0 copy-done
  8.4 0.3 reshape.88
  8.7 0.2 copy.13
  9.1 0.1 copy.18
  9.2 0.1 reshape.92
  9.3 0.1 pad_maximum_fusion
  9.4 36.3 %all_to_all.5 = bf16[32,134,128]{2,1,0:T(8,128)(2,1)S(1)} all-to-all(bf16[32,134,128]{2,1,0:T(8,128)(2,1)S(1)} %pad_maximum_fusion), channel_id=1, replica_groups=mesh['ctx'=4,'row'=8] {'row','ctx'}, dimensions={0} | all-to-all | bytes 2195456 | tf_op jit(solution)/shard_map/all_to_all | solution.py:143
  45.7 0.2 reshape.91
  46.1 0.1 sub.44
  46.2 0.1 squeeze.11
  46.3 0.7 %multiply_reduce_fusion = f32[8,128,128]{2,1,0:T(8,128)S(1)} fusion(bf16[8,4,134,128]{3,2,1,0:T(8,128)(2,1)S(1)} %bitcast.35, f32[8,4,128]{2,1,0:T(4,128)S(1)} %subtract_exponential_fusion), kind=kLoop, calls=%fused_computation | loop fusion | flops 1441792 | bytes 1589248 | tf_op jit(solution)/shard_map/reduce_sum | solution.py:155
  47.0 0.2 divide_convert_fusion
  47.3 0.1 copy.17
  47.4 0.7 %copy.24 = bf16[32,8,4,128]{3,1,2,0:T(8,128)(2,1)} copy(bf16[32,8,4,128]{3,2,1,0:T(4,128)(2,1)S(1)} %bitcast.40) | data formatting | bytes 524288
  (8 shorter events, 0.3 us)
Async XLA Ops:
  6.9 1.5 %copy-start = (f32[2,16,256]{2,1,0:T(8,128)S(1)}, f32[2,16,256]{2,1,0:T(8,128)}, u32[]{:S(2)}) copy-start(f32[2,16,256]{2,1,0:T(8,128)} %get-tuple-element.8) | copy-start | bytes 98308

commit v13 on v12

--- a/solution.py
+++ b/solution.py
@@ -10,7 +10,7 @@
 HEADS = 16
 HEAD_DIM = 128
 BLOCK = 128
-HEADS_PER_STEP = 8
+HEADS_PER_STEP = 16
 
 
 masked_fill = -1e30

time: 48.3 us -> 48.3 us (level)
  no operation moved by 1% of the time
where the time goes in v13:
time: 48.3 us; the launch traced here: 48.2 us
  blocking collectives  36.3 us (75%)
  Pallas kernels  6.96 us (14%)
  local copies, waits for them, and re-layouts  3.54 us (7%)
  other arithmetic  1.27 us (3%)
    all_to_all x1, blocking collectives, local(): arrived = lax.all_to_all(payload, ('row', 'ctx'), 0, 0, tiled=True)  36.3 us
    pallas_call x1, Pallas kernels, local_attention(): pl.pallas_call(functools.partial(attention_kernel, shape), grid_spec=grid...  6.96 us
    reshape x1, local copies, waits for them, and re-layouts, local(): part_low = part.reshape(shards, head_share, per_owner, owners, HEAD_DIM)  1.47 us

profile of v13, /device:TPU:0, one launch (start us, length us, event | category | flops | bytes accessed | tf_op | source)
XLA Modules:
  0.0 48.2 jit_solution(5736235047375095923)
XLA Ops:
  0.0 7.0 %shard_map.55 = (bf16[16,256,128]{2,1,0:T(8,128)(2,1)}, f32[2,16,256]{2,1,0:T(8,128)}) custom-call(s32[2,8]{1,0:T(2,128)} %list_ref.1, s32[2]{0:T(128)} %count_ref.1, s32[1]{0:T(128)} %bitcast.first_ref, bf16[256,2048]{1,0:T(8,128)(2,1)} %q_ref.1, bf16[384,2048]{1,0:T(8,128)(2,1)} %k_ref.1, bf16[384,2048]{1,0:T(8,128)(2,1)} %v_ref.1), custom_call_target="tpu_custom_call" | custom-call | flops 805306368 | bytes 5242880 | tf_op jit(solution)/shard_map/pallas_call | solution.py:88
  7.0 0.0 copy-start
  7.0 1.5 %copy.12 = bf16[4,4,32,8,128]{4,2,1,0,3:T(8,128)(2,1)S(1)} copy(bf16[4,4,32,8,128]{4,3,2,1,0:T(8,128)(2,1)} %bitcast.39) | data formatting | bytes 2097152 | tf_op jit(solution)/shard_map/reshape | solution.py:130
  8.4 0.0 copy-done
  8.4 0.3 reshape.88
  8.8 0.2 copy.13
  9.1 0.1 copy.18
  9.2 0.1 reshape.92
  9.3 0.1 pad_maximum_fusion
  9.4 36.3 %all_to_all.5 = bf16[32,134,128]{2,1,0:T(8,128)(2,1)S(1)} all-to-all(bf16[32,134,128]{2,1,0:T(8,128)(2,1)S(1)} %pad_maximum_fusion), channel_id=1, replica_groups=mesh['ctx'=4,'row'=8] {'row','ctx'}, dimensions={0} | all-to-all | bytes 2195456 | tf_op jit(solution)/shard_map/all_to_all | solution.py:143
  45.7 0.2 reshape.91
  46.1 0.1 sub.44
  46.2 0.1 squeeze.11
  46.3 0.7 %multiply_reduce_fusion = f32[8,128,128]{2,1,0:T(8,128)S(1)} fusion(bf16[8,4,134,128]{3,2,1,0:T(8,128)(2,1)S(1)} %bitcast.35, f32[8,4,128]{2,1,0:T(4,128)S(1)} %subtract_exponential_fusion), kind=kLoop, calls=%fused_computation | loop fusion | flops 1441792 | bytes 1589248 | tf_op jit(solution)/shard_map/reduce_sum | solution.py:155
  47.1 0.2 divide_convert_fusion
  47.3 0.1 copy.17
  47.4 0.7 %copy.24 = bf16[32,8,4,128]{3,1,2,0:T(8,128)(2,1)} copy(bf16[32,8,4,128]{3,2,1,0:T(4,128)(2,1)S(1)} %bitcast.40) | data formatting | bytes 524288
  (8 shorter events, 0.3 us)
Async XLA Ops:
  7.0 1.5 %copy-start = (f32[2,16,256]{2,1,0:T(8,128)S(1)}, f32[2,16,256]{2,1,0:T(8,128)}, u32[]{:S(2)}) copy-start(f32[2,16,256]{2,1,0:T(8,128)} %get-tuple-element.8) | copy-start | bytes 98308

commit v14 on v13

--- a/solution.py
+++ b/solution.py
@@ -54,8 +54,13 @@
             preferred_element_type=jnp.float32,
         )
         part_ref[hl] = seg_out.astype(jnp.bfloat16)
-        stat_ref[0, hl : hl + 1, :] = seg_max
-        stat_ref[1, hl : hl + 1, :] = seg_total
+        for kind, value in enumerate((seg_max, seg_total)):
+            hi = value.astype(jnp.bfloat16)
+            rest = value - hi.astype(jnp.float32)
+            mid = rest.astype(jnp.bfloat16)
+            lo = (rest - mid.astype(jnp.float32)).astype(jnp.bfloat16)
+            for part, piece in enumerate((hi, mid, lo)):
+                stat_ref[part, kind, hl : hl + 1, :] = piece
 
 
 def local_attention(queries, keys, values, block_list, block_count, first_block, shards):
@@ -77,7 +82,7 @@
         ],
         out_specs=[
             pl.BlockSpec((step_heads, rows, HEAD_DIM), lambda g, *_: (g, 0, 0)),
-            pl.BlockSpec((2, step_heads, rows), lambda g, *_: (0, g, 0)),
+            pl.BlockSpec((3, 2, step_heads, rows), lambda g, *_: (0, 0, g, 0)),
         ],
         scratch_shapes=[
             pltpu.VMEM((ctx_span, rows), jnp.float32),
@@ -90,7 +95,7 @@
         grid_spec=grid_spec,
         out_shape=[
             jax.ShapeDtypeStruct((HEADS, rows, HEAD_DIM), jnp.bfloat16),
-            jax.ShapeDtypeStruct((2, HEADS, rows), jnp.float32),
+            jax.ShapeDtypeStruct((3, 2, HEADS, rows), jnp.bfloat16),
         ],
         compiler_params=pltpu.CompilerParams(dimension_semantics=("arbitrary",)),
         cost_estimate=pl.CostEstimate(
@@ -131,11 +136,10 @@
     part_low = jnp.transpose(part_low, (3, 0, 1, 2, 4)).reshape(
         owners * shards, head_share * per_owner, HEAD_DIM
     )
-    stats = jnp.transpose(stat.reshape(2, shards, head_share, per_owner, owners), (4, 1, 0, 2, 3))
-    stats = stats.reshape(owners * shards, 2, head_share, per_owner)
+    stats = jnp.transpose(stat.reshape(3, 2, shards, head_share, per_owner, owners), (5, 2, 0, 1, 3, 4))
     stat_count = 3 * 2 * head_share * per_owner
     stat_rows = -(-stat_count // HEAD_DIM)
-    stat_low = split_three(stats).reshape(owners * shards, stat_count)
+    stat_low = stats.reshape(owners * shards, stat_count)
     stat_low = jnp.pad(stat_low, ((0, 0), (0, stat_rows * HEAD_DIM - stat_count)))
     payload = jnp.concatenate(
         [part_low, stat_low.reshape(owners * shards, stat_rows, HEAD_DIM)], axis=1

time: 48.3 us -> 49 us (1.014)
  local copies, waits for them, and re-layouts: 3.54 us -> 4.27 us
    reshape x1 -> x3, local copies, waits for them, and re-layouts: 0.31 us -> 1.49 us  [the longest x1 0.92 us: local(): stat.reshape(3, 2, shards, head_share, per_owner, owners)]
where the time goes in v14:
time: 49 us; the launch traced here: 48.8 us
  blocking collectives  36.3 us (74%)
  Pallas kernels  7 us (14%)
  local copies, waits for them, and re-layouts  4.27 us (9%)
  other arithmetic  1.18 us (2%)
    all_to_all x1, blocking collectives, local(): arrived = lax.all_to_all(payload, ('row', 'ctx'), 0, 0, tiled=True)  36.3 us
    pallas_call x1, Pallas kernels, local_attention(): pl.pallas_call(functools.partial(attention_kernel, shape), grid_spec=grid...  7 us
    reshape x1, local copies, waits for them, and re-layouts, local(): part_low = part.reshape(shards, head_share, per_owner, owners, HEAD_DIM)  1.47 us

profile of v14, /device:TPU:0, one launch (start us, length us, event | category | flops | bytes accessed | tf_op | source)
XLA Modules:
  0.0 48.8 jit_solution(16264688646508525363)
XLA Ops:
  0.0 7.0 %shard_map.55 = (bf16[16,256,128]{2,1,0:T(8,128)(2,1)}, bf16[3,2,16,256]{3,2,1,0:T(8,128)(2,1)}) custom-call(s32[2,8]{1,0:T(2,128)} %list_ref.1, s32[2]{0:T(128)} %count_ref.1, s32[1]{0:T(128)} %bitcast.first_ref, bf16[256,2048]{1,0:T(8,128)(2,1)} %q_ref.1, bf16[384,2048]{1,0:T(8,128)(2,1)} %k_ref.1, bf16[384,2048]{1,0:T(8,128)(2,1)} %v_ref.1), custom_call_target="tpu_custom_call" | custom-call | flops 805306368 | bytes 5242880 | tf_op jit(solution)/shard_map/pallas_call | solution.py:93
  7.0 0.0 copy-start
  7.0 1.5 %copy.11 = bf16[4,4,32,8,128]{4,2,1,0,3:T(8,128)(2,1)S(1)} copy(bf16[4,4,32,8,128]{4,3,2,1,0:T(8,128)(2,1)} %bitcast.40) | data formatting | bytes 2097152 | tf_op jit(solution)/shard_map/reshape | solution.py:135
  8.5 0.0 copy-done
  8.5 0.9 %reshape.46 = bf16[3,2,4,4,32,8]{5,4,3,2,1,0:T(8,128)(2,1)S(1)} reshape(bf16[3,2,16,256]{3,2,1,0:T(8,128)(2,1)S(1)} %copy-done) | data formatting | bytes 98304 | tf_op jit(solution)/shard_map/reshape | solution.py:139
  9.4 0.4 copy.16
  9.8 0.1 reshape.50
  10.0 0.1 pad_maximum_fusion
  10.1 36.3 %all_to_all.5 = bf16[32,134,128]{2,1,0:T(8,128)(2,1)S(1)} all-to-all(bf16[32,134,128]{2,1,0:T(8,128)(2,1)S(1)} %pad_maximum_fusion), channel_id=1, replica_groups=mesh['ctx'=4,'row'=8] {'row','ctx'}, dimensions={0} | all-to-all | bytes 2195456 | tf_op jit(solution)/shard_map/all_to_all | solution.py:147
  46.4 0.2 reshape.49
  46.8 0.1 sub.18
  46.9 0.1 squeeze.11
  47.0 0.7 %multiply_reduce_fusion = f32[8,128,128]{2,1,0:T(8,128)S(1)} fusion(bf16[8,4,134,128]{3,2,1,0:T(8,128)(2,1)S(1)} %bitcast.36, f32[8,4,128]{2,1,0:T(4,128)S(1)} %subtract_exponential_fusion), kind=kLoop, calls=%fused_computation | loop fusion | flops 1441792 | bytes 1589248 | tf_op jit(solution)/shard_map/reduce_sum | solution.py:159
  47.7 0.2 divide_convert_fusion
  47.9 0.1 copy.15
  48.1 0.7 %copy.22 = bf16[32,8,4,128]{3,1,2,0:T(8,128)(2,1)} copy(bf16[32,8,4,128]{3,2,1,0:T(4,128)(2,1)S(1)} %bitcast.41) | data formatting | bytes 524288
  (6 shorter events, 0.2 us)
Async XLA Ops:
  7.0 1.5 %copy-start = (bf16[3,2,16,256]{3,2,1,0:T(8,128)(2,1)S(1)}, bf16[3,2,16,256]{3,2,1,0:T(8,128)(2,1)}, u32[]{:S(2)}) copy-start(bf16[3,2,16,256]{3,2,1,0:T(8,128)(2,1)} %get-tuple-element.8) | copy-start | bytes 147460

commit v15 on v13

--- a/solution.py
+++ b/solution.py
@@ -17,33 +17,39 @@
 
 
 def attention_kernel(shape, list_ref, count_ref, first_ref, q_ref, k_ref, v_ref, part_ref, stat_ref,
-                     bias_ref, dead_ref):
-    rows, head_share, q_blocks, k_blocks, max_sel = shape
+                     bias_ref, dead_ref, q_scr):
+    rows, owners, per_owner, head_share, q_blocks, k_blocks, max_sel = shape
 
     @pl.when(pl.program_id(0) == 0)
     def _():
         first = first_ref[0]
+        pos = lax.broadcasted_iota(jnp.int32, (8, rows), 1)
+        q_block = ((pos % per_owner) * owners + pos // per_owner) // BLOCK
+        dead = jnp.full((8, rows), jnp.inf, jnp.float32)
+        biases = [jnp.full((8, rows), masked_fill, jnp.float32) for _ in range(k_blocks)]
         for a in range(q_blocks):
-            any_live = jnp.int32(0)
             for b in range(k_blocks):
                 hit = jnp.int32(0)
                 for slot in range(max_sel):
                     found = (list_ref[a, slot] == first + b) & (slot < count_ref[a])
                     hit = jnp.maximum(hit, jnp.where(found, 1, 0).astype(jnp.int32))
-                any_live = jnp.maximum(any_live, hit)
-                bias = jnp.where(hit > 0, 0.0, masked_fill).astype(jnp.float32)
-                bias_ref[b * BLOCK : (b + 1) * BLOCK, a * BLOCK : (a + 1) * BLOCK] = jnp.full(
-                    (BLOCK, BLOCK), bias, jnp.float32
-                )
-            dead = jnp.where(any_live > 0, 0.0, jnp.inf).astype(jnp.float32)
-            dead_ref[:, a * BLOCK : (a + 1) * BLOCK] = jnp.full((8, BLOCK), dead, jnp.float32)
+                live = (q_block == a) & (hit > 0)
+                biases[b] = jnp.where(live, 0.0, biases[b])
+                dead = jnp.where(live, 0.0, dead)
+        for b in range(k_blocks):
+            bias_ref[b * BLOCK : (b + 1) * BLOCK, :] = jnp.broadcast_to(biases[b][0:1, :], (BLOCK, rows))
+        dead_ref[...] = dead
 
     score_scale = 1.0 / HEAD_DIM**0.5
     dead_row = dead_ref[0:1, :]
     for hl in range(head_share):
         cols = slice(hl * HEAD_DIM, (hl + 1) * HEAD_DIM)
+        q_scr[...] = q_ref[:, cols].astype(jnp.float32)
+        q_perm = jnp.concatenate(
+            [q_scr[pl.ds(r, per_owner, stride=owners), :] for r in range(owners)], axis=0
+        ).astype(jnp.bfloat16)
         scores = lax.dot_general(
-            k_ref[:, cols], q_ref[:, cols], (((1,), (1,)), ((), ())), preferred_element_type=jnp.float32
+            k_ref[:, cols], q_perm, (((1,), (1,)), ((), ())), preferred_element_type=jnp.float32
         )
         scores = scores * score_scale + bias_ref[...]
         seg_max = jnp.max(scores, axis=0, keepdims=True)
@@ -58,15 +64,16 @@
         stat_ref[1, hl : hl + 1, :] = seg_total
 
 
-def local_attention(queries, keys, values, block_list, block_count, first_block, shards):
+def local_attention(queries, keys, values, block_list, block_count, first_block, owners, shards):
     rows = queries.shape[0]
+    per_owner = rows // owners
     ctx_span = keys.shape[0]
     step_heads = HEADS_PER_STEP
     step_width = step_heads * HEAD_DIM
     q_blocks = rows // BLOCK
     k_blocks = ctx_span // BLOCK
     max_sel = block_list.shape[1]
-    shape = (rows, step_heads, q_blocks, k_blocks, max_sel)
+    shape = (rows, owners, per_owner, step_heads, q_blocks, k_blocks, max_sel)
     grid_spec = pltpu.PrefetchScalarGridSpec(
         num_scalar_prefetch=3,
         grid=(HEADS // step_heads,),
@@ -82,6 +89,7 @@
         scratch_shapes=[
             pltpu.VMEM((ctx_span, rows), jnp.float32),
             pltpu.VMEM((8, rows), jnp.float32),
+            pltpu.VMEM((rows, HEAD_DIM), jnp.float32),
         ],
     )
     flops = 4 * HEADS * rows * ctx_span * HEAD_DIM
@@ -125,13 +133,13 @@
     blocks_here = ctx_span // BLOCK
     first_block = (lax.axis_index("ctx") * blocks_here).astype(jnp.int32).reshape(1)
     part, stat = local_attention(
-        queries, keys, values, block_list.astype(jnp.int32), block_count.astype(jnp.int32), first_block, shards
+        queries, keys, values, block_list.astype(jnp.int32), block_count.astype(jnp.int32), first_block, owners, shards
     )
-    part_low = part.reshape(shards, head_share, per_owner, owners, HEAD_DIM)
-    part_low = jnp.transpose(part_low, (3, 0, 1, 2, 4)).reshape(
+    part_low = part.reshape(shards, head_share, owners, per_owner, HEAD_DIM)
+    part_low = jnp.transpose(part_low, (2, 0, 1, 3, 4)).reshape(
         owners * shards, head_share * per_owner, HEAD_DIM
     )
-    stats = jnp.transpose(stat.reshape(2, shards, head_share, per_owner, owners), (4, 1, 0, 2, 3))
+    stats = jnp.transpose(stat.reshape(2, shards, head_share, owners, per_owner), (3, 1, 0, 2, 4))
     stats = stats.reshape(owners * shards, 2, head_share, per_owner)
     stat_count = 3 * 2 * head_share * per_owner
     stat_rows = -(-stat_count // HEAD_DIM)

time: 48.3 us -> 48.3 us (level)
    reshape x2 -> x3, local copies, waits for them, and re-layouts: 1.77 us -> 1.53 us  [the longest x1 1.36 us: local(): part_low = part.reshape(shards, head_share, owners, per_owner, HEAD_DIM)]
where the time goes in v15:
time: 48.3 us; the launch traced here: 48.1 us
  blocking collectives  36.3 us (75%)
  Pallas kernels  7.37 us (15%)
  local copies, waits for them, and re-layouts  3.09 us (6%)
  other arithmetic  1.26 us (3%)
    all_to_all x1, blocking collectives, local(): arrived = lax.all_to_all(payload, ('row', 'ctx'), 0, 0, tiled=True)  36.3 us
    pallas_call x1, Pallas kernels, local_attention(): pl.pallas_call(functools.partial(attention_kernel, shape), grid_spec=grid...  7.37 us
    reshape x1, local copies, waits for them, and re-layouts, local(): part_low = part.reshape(shards, head_share, owners, per_owner, HEAD_DIM)  1.36 us

profile of v15, /device:TPU:0, one launch (start us, length us, event | category | flops | bytes accessed | tf_op | source)
XLA Modules:
  0.0 48.1 jit_solution(1715306441147012718)
XLA Ops:
  0.0 7.4 %shard_map.55 = (bf16[16,256,128]{2,1,0:T(8,128)(2,1)}, f32[2,16,256]{2,1,0:T(8,128)}) custom-call(s32[2,8]{1,0:T(2,128)} %list_ref.1, s32[2]{0:T(128)} %count_ref.1, s32[1]{0:T(128)} %bitcast.first_ref, bf16[256,2048]{1,0:T(8,128)(2,1)} %q_ref.1, bf16[384,2048]{1,0:T(8,128)(2,1)} %k_ref.1, bf16[384,2048]{1,0:T(8,128)(2,1)} %v_ref.1), custom_call_target="tpu_custom_call" | custom-call | flops 805306368 | bytes 5242880 | tf_op jit(solution)/shard_map/pallas_call | solution.py:96
  7.4 0.0 copy-start
  7.4 1.4 %copy.12 = bf16[4,4,8,32,128]{4,3,1,0,2:T(8,128)(2,1)S(1)} copy(bf16[4,4,8,32,128]{4,3,2,1,0:T(8,128)(2,1)} %bitcast.39) | data formatting | bytes 2097152 | tf_op jit(solution)/shard_map/reshape | solution.py:138
  8.7 0.0 copy-done
  8.7 0.1 reshape.88
  8.8 0.1 copy.13
  9.0 0.1 copy.18
  9.1 0.1 reshape.92
  9.3 0.1 pad_maximum_fusion
  9.4 36.3 %all_to_all.5 = bf16[32,134,128]{2,1,0:T(8,128)(2,1)S(1)} all-to-all(bf16[32,134,128]{2,1,0:T(8,128)(2,1)S(1)} %pad_maximum_fusion), channel_id=1, replica_groups=mesh['ctx'=4,'row'=8] {'row','ctx'}, dimensions={0} | all-to-all | bytes 2195456 | tf_op jit(solution)/shard_map/all_to_all | solution.py:151
  45.7 0.2 reshape.91
  46.1 0.1 sub.44
  46.2 0.1 squeeze.11
  46.3 0.7 %multiply_reduce_fusion = f32[8,128,128]{2,1,0:T(8,128)S(1)} fusion(bf16[8,4,134,128]{3,2,1,0:T(8,128)(2,1)S(1)} %bitcast.36, f32[8,4,128]{2,1,0:T(4,128)S(1)} %subtract_exponential_fusion), kind=kLoop, calls=%fused_computation | loop fusion | flops 1441792 | bytes 1589248 | tf_op jit(solution)/shard_map/reduce_sum | solution.py:163
  47.0 0.2 divide_convert_fusion
  47.2 0.1 copy.17
  47.4 0.7 %copy.24 = bf16[32,8,4,128]{3,1,2,0:T(8,128)(2,1)} copy(bf16[32,8,4,128]{3,2,1,0:T(4,128)(2,1)S(1)} %bitcast.40) | data formatting | bytes 524288
  (8 shorter events, 0.3 us)
Async XLA Ops:
  7.4 1.4 %copy-start = (f32[2,16,256]{2,1,0:T(8,128)S(1)}, f32[2,16,256]{2,1,0:T(8,128)}, u32[]{:S(2)}) copy-start(f32[2,16,256]{2,1,0:T(8,128)} %get-tuple-element.8) | copy-start | bytes 98308

commit v16 on v15

--- a/solution.py
+++ b/solution.py
@@ -59,7 +59,7 @@
             probs.astype(jnp.bfloat16), v_ref[:, cols], (((0,), (0,)), ((), ())),
             preferred_element_type=jnp.float32,
         )
-        part_ref[hl] = seg_out.astype(jnp.bfloat16)
+        part_ref[:, hl] = seg_out.reshape(owners, per_owner, HEAD_DIM).astype(jnp.bfloat16)
         stat_ref[0, hl : hl + 1, :] = seg_max
         stat_ref[1, hl : hl + 1, :] = seg_total
 
@@ -83,7 +83,7 @@
             pl.BlockSpec((ctx_span, step_width), lambda g, *_: (0, g)),
         ],
         out_specs=[
-            pl.BlockSpec((step_heads, rows, HEAD_DIM), lambda g, *_: (g, 0, 0)),
+            pl.BlockSpec((owners, step_heads, per_owner, HEAD_DIM), lambda g, *_: (0, g, 0, 0)),
             pl.BlockSpec((2, step_heads, rows), lambda g, *_: (0, g, 0)),
         ],
         scratch_shapes=[
@@ -97,7 +97,7 @@
         functools.partial(attention_kernel, shape),
         grid_spec=grid_spec,
         out_shape=[
-            jax.ShapeDtypeStruct((HEADS, rows, HEAD_DIM), jnp.bfloat16),
+            jax.ShapeDtypeStruct((owners, HEADS, per_owner, HEAD_DIM), jnp.bfloat16),
             jax.ShapeDtypeStruct((2, HEADS, rows), jnp.float32),
         ],
         compiler_params=pltpu.CompilerParams(dimension_semantics=("arbitrary",)),
@@ -135,10 +135,7 @@
     part, stat = local_attention(
         queries, keys, values, block_list.astype(jnp.int32), block_count.astype(jnp.int32), first_block, owners, shards
     )
-    part_low = part.reshape(shards, head_share, owners, per_owner, HEAD_DIM)
-    part_low = jnp.transpose(part_low, (2, 0, 1, 3, 4)).reshape(
-        owners * shards, head_share * per_owner, HEAD_DIM
-    )
+    part_low = part.reshape(owners * shards, head_share * per_owner, HEAD_DIM)
     stats = jnp.transpose(stat.reshape(2, shards, head_share, owners, per_owner), (3, 1, 0, 2, 4))
     stats = stats.reshape(owners * shards, 2, head_share, per_owner)
     stat_count = 3 * 2 * head_share * per_owner

time: 48.3 us -> 49.4 us (1.023)
  other arithmetic: 1.26 us -> 2.38 us
    reshape x1 -> x0, local copies, waits for them, and re-layouts: 1.36 us -> none  [local(): part_low = part.reshape(shards, head_share, owners, per_owner, HEAD_DIM)]
    reduce_sum x1, other arithmetic: 0.73 us -> 1.86 us  [local(): numerator = jnp.sum(part_in.astype(jnp.float32) * weight[..., None], axis=1)]
    reshape x2, local copies, waits for them, and re-layouts: 0.17 us -> 1.02 us  [local(): stat.reshape(2, shards, head_share, owners, per_owner)]
where the time goes in v16:
time: 49.4 us; the launch traced here: 49.3 us
  blocking collectives  36.3 us (73%)
  Pallas kernels  7.37 us (15%)
  local copies, waits for them, and re-layouts  3.09 us (6%)
  other arithmetic  2.38 us (5%)
    all_to_all x1, blocking collectives, local(): arrived = lax.all_to_all(payload, ('row', 'ctx'), 0, 0, tiled=True)  36.3 us
    pallas_call x1, Pallas kernels, local_attention(): pl.pallas_call(functools.partial(attention_kernel, shape), grid_spec=grid...  7.37 us
    reduce_sum x1, other arithmetic, local(): numerator = jnp.sum(part_in.astype(jnp.float32) * weight[..., None], axis=1)  1.86 us
    reshape x2, local copies, waits for them, and re-layouts, local(): stat.reshape(2, shards, head_share, owners, per_owner)  1.02 us

profile of v16, /device:TPU:0, one launch (start us, length us, event | category | flops | bytes accessed | tf_op | source)
XLA Modules:
  0.0 49.3 jit_solution(5460062059473573397)
XLA Ops:
  0.0 7.4 %shard_map.55 = (bf16[8,16,32,128]{3,2,1,0:T(8,128)(2,1)}, f32[2,16,256]{2,1,0:T(8,128)}) custom-call(s32[2,8]{1,0:T(2,128)} %list_ref.1, s32[2]{0:T(128)} %count_ref.1, s32[1]{0:T(128)} %bitcast.first_ref, bf16[256,2048]{1,0:T(8,128)(2,1)} %q_ref.1, bf16[384,2048]{1,0:T(8,128)(2,1)} %k_ref.1, bf16[384,2048]{1,0:T(8,128)(2,1)} %v_ref.1), custom_call_target="tpu_custom_call" | custom-call | flops 805306368 | bytes 5242880 | tf_op jit(solution)/shard_map/pallas_call | solution.py:96
  7.4 0.0 copy-start
  7.4 0.9 %reshape.84 = f32[2,4,4,8,32]{4,3,2,1,0:T(8,128)S(1)} reshape(f32[2,16,256]{2,1,0:T(8,128)} %get-tuple-element.8) | data formatting | bytes 65536 | tf_op jit(solution)/shard_map/reshape | solution.py:139
  8.3 0.1 copy.28
  8.5 0.1 copy.37
  8.6 0.1 reshape.88
  8.8 0.0 copy-done
  8.8 0.1 pad_maximum_fusion
  8.9 36.3 %all_to_all.5 = bf16[32,134,128]{2,1,0:T(8,128)(2,1)S(1)} all-to-all(bf16[32,134,128]{2,1,0:T(8,128)(2,1)S(1)} %pad_maximum_fusion), channel_id=1, replica_groups=mesh['ctx'=4,'row'=8] {'row','ctx'}, dimensions={0} | all-to-all | bytes 2195456 | tf_op jit(solution)/shard_map/all_to_all | solution.py:148
  45.2 0.2 copy.31
  45.3 0.2 reshape.87
  45.7 0.1 reshape.89
  45.8 0.1 sub.44
  45.9 0.3 copy.33
  46.2 1.9 %multiply_reduce_fusion = f32[8,128,128]{2,0,1:T(8,128)S(1)} fusion(bf16[8,4,134,128]{3,1,0,2:T(4,128)(2,1)S(1)} %bitcast.33, f32[8,4,128]{1,0,2:T(8,128)S(1)} %copy.33), kind=kLoop, calls=%fused_computation | loop fusion | flops 1441792 | bytes 1589248 | tf_op jit(solution)/shard_map/reduce_sum | solution.py:160
  48.1 0.1 copy.34
  48.2 0.2 divide_convert_fusion
  48.4 0.1 copy.36
  48.5 0.7 %copy.52 = bf16[32,8,4,128]{3,1,2,0:T(8,128)(2,1)} copy(bf16[32,8,4,128]{3,2,1,0:T(4,128)(2,1)S(1)} %bitcast.36) | data formatting | bytes 524288
  (7 shorter events, 0.2 us)
Async XLA Ops:
  7.4 1.4 %copy-start = (bf16[8,16,32,128]{3,2,1,0:T(8,128)(2,1)S(1)}, bf16[8,16,32,128]{3,2,1,0:T(8,128)(2,1)}, u32[]{:S(2)}) copy-start(bf16[8,16,32,128]{3,2,1,0:T(8,128)(2,1)} %get-tuple-element.7) | copy-start | bytes 3145732

commit v17 on v16

--- a/solution.py
+++ b/solution.py
@@ -5,6 +5,7 @@
 from jax import lax
 from jax.experimental import pallas as pl
 from jax.experimental.pallas import tpu as pltpu
+from jax.experimental.layout import Layout, with_layout_constraint
 from jax.sharding import PartitionSpec as P
 
 HEADS = 16
@@ -146,6 +147,7 @@
         [part_low, stat_low.reshape(owners * shards, stat_rows, HEAD_DIM)], axis=1
     )
     arrived = lax.all_to_all(payload, ("row", "ctx"), 0, 0, tiled=True)
+    arrived = with_layout_constraint(arrived, Layout(major_to_minor=(0, 1, 2)))
     arrived = arrived.reshape(owners, shards, head_share * per_owner + stat_rows, HEAD_DIM)
     part_in = arrived[:, :, : head_share * per_owner].reshape(owners, shards, head_share, per_owner, HEAD_DIM)
     stat_in = arrived[:, :, head_share * per_owner :].reshape(owners * shards, stat_rows * HEAD_DIM)

time: 49.4 us -> 47.8 us (0.968)
  other arithmetic: 2.38 us -> 1.44 us
  local copies, waits for them, and re-layouts: 3.09 us -> 2.45 us
    reduce_sum x1, other arithmetic: 1.86 us -> 0.73 us  [local(): numerator = jnp.sum(part_in.astype(jnp.float32) * weight[..., None], axis=1)]
    reshape x2 -> x1, local copies, waits for them, and re-layouts: 1.02 us -> 0.93 us  [local(): stat.reshape(2, shards, head_share, owners, per_owner)]
where the time goes in v17:
time: 47.8 us; the launch traced here: 47.7 us
  blocking collectives  36.3 us (76%)
  Pallas kernels  7.37 us (15%)
  local copies, waits for them, and re-layouts  2.45 us (5%)
  other arithmetic  1.44 us (3%)
    all_to_all x1, blocking collectives, local(): arrived = lax.all_to_all(payload, ('row', 'ctx'), 0, 0, tiled=True)  36.3 us
    pallas_call x1, Pallas kernels, local_attention(): pl.pallas_call(functools.partial(attention_kernel, shape), grid_spec=grid...  7.37 us

profile of v17, /device:TPU:0, one launch (start us, length us, event | category | flops | bytes accessed | tf_op | source)
XLA Modules:
  0.0 47.7 jit_solution(17899641620872885501)
XLA Ops:
  0.0 7.4 %shard_map.55 = (bf16[8,16,32,128]{3,2,1,0:T(8,128)(2,1)}, f32[2,16,256]{2,1,0:T(8,128)}) custom-call(s32[2,8]{1,0:T(2,128)} %list_ref.1, s32[2]{0:T(128)} %count_ref.1, s32[1]{0:T(128)} %bitcast.first_ref, bf16[256,2048]{1,0:T(8,128)(2,1)} %q_ref.1, bf16[384,2048]{1,0:T(8,128)(2,1)} %k_ref.1, bf16[384,2048]{1,0:T(8,128)(2,1)} %v_ref.1), custom_call_target="tpu_custom_call" | custom-call | flops 805306368 | bytes 5242880 | tf_op jit(solution)/shard_map/pallas_call | solution.py:97
  7.4 0.0 copy-start
  7.4 0.9 %reshape.84 = f32[2,4,4,8,32]{4,3,2,1,0:T(8,128)S(1)} reshape(f32[2,16,256]{2,1,0:T(8,128)} %get-tuple-element.8) | data formatting | bytes 65536 | tf_op jit(solution)/shard_map/reshape | solution.py:140
  8.4 0.1 reduce-precision_convert_fusion.1
  8.4 0.2 pad_maximum_fusion.1
  8.6 0.1 convert_element_type.21
  8.8 0.0 copy-done
  8.8 0.1 pad_maximum_fusion
  8.9 36.3 %all_to_all.5 = bf16[32,134,128]{2,1,0:T(8,128)(2,1)S(1)} all-to-all(bf16[32,134,128]{2,1,0:T(8,128)(2,1)S(1)} %pad_maximum_fusion), channel_id=1, replica_groups=mesh['ctx'=4,'row'=8] {'row','ctx'}, dimensions={0} | all-to-all | bytes 2195456 | tf_op jit(solution)/shard_map/all_to_all | solution.py:149
  45.2 0.2 reshape.87
  45.6 0.1 sub.44
  45.7 0.1 squeeze.11
  45.8 0.7 %multiply_reduce_fusion = f32[8,128,128]{2,1,0:T(8,128)S(1)} fusion(bf16[8,4,134,128]{3,2,1,0:T(8,128)(2,1)S(1)} %bitcast.34, f32[8,4,128]{2,1,0:T(4,128)S(1)} %subtract_exponential_fusion), kind=kLoop, calls=%fused_computation | loop fusion | flops 1441792 | bytes 1589248 | tf_op jit(solution)/shard_map/reduce_sum | solution.py:162
  46.6 0.2 divide_convert_fusion
  46.8 0.1 copy.14
  46.9 0.7 %copy.19 = bf16[32,8,4,128]{3,1,2,0:T(8,128)(2,1)} copy(bf16[32,8,4,128]{3,2,1,0:T(4,128)(2,1)S(1)} %bitcast.37) | data formatting | bytes 524288
  (8 shorter events, 0.2 us)
Async XLA Ops:
  7.4 1.4 %copy-start = (bf16[8,16,32,128]{3,2,1,0:T(8,128)(2,1)S(1)}, bf16[8,16,32,128]{3,2,1,0:T(8,128)(2,1)}, u32[]{:S(2)}) copy-start(bf16[8,16,32,128]{3,2,1,0:T(8,128)(2,1)} %get-tuple-element.7) | copy-start | bytes 3145732

commit v18 on v17

--- a/solution.py
+++ b/solution.py
@@ -11,7 +11,7 @@
 HEADS = 16
 HEAD_DIM = 128
 BLOCK = 128
-HEADS_PER_STEP = 16
+HEADS_PER_STEP = 8
 
 
 masked_fill = -1e30

time: 47.8 us -> 47.8 us (level)
  no operation moved by 1% of the time
where the time goes in v18:
time: 47.8 us; the launch traced here: 47.7 us
  blocking collectives  36.3 us (76%)
  Pallas kernels  7.38 us (15%)
  local copies, waits for them, and re-layouts  2.45 us (5%)
  other arithmetic  1.44 us (3%)
    all_to_all x1, blocking collectives, local(): arrived = lax.all_to_all(payload, ('row', 'ctx'), 0, 0, tiled=True)  36.3 us
    pallas_call x1, Pallas kernels, local_attention(): pl.pallas_call(functools.partial(attention_kernel, shape), grid_spec=grid...  7.38 us

profile of v18, /device:TPU:0, one launch (start us, length us, event | category | flops | bytes accessed | tf_op | source)
XLA Modules:
  0.0 47.7 jit_solution(4763976841272806685)
XLA Ops:
  0.0 7.4 %shard_map.55 = (bf16[8,16,32,128]{3,2,1,0:T(8,128)(2,1)}, f32[2,16,256]{2,1,0:T(8,128)}) custom-call(s32[2,8]{1,0:T(2,128)} %list_ref.1, s32[2]{0:T(128)} %count_ref.1, s32[1]{0:T(128)} %bitcast.first_ref, bf16[256,2048]{1,0:T(8,128)(2,1)} %q_ref.1, bf16[384,2048]{1,0:T(8,128)(2,1)} %k_ref.1, bf16[384,2048]{1,0:T(8,128)(2,1)} %v_ref.1), custom_call_target="tpu_custom_call" | custom-call | flops 805306368 | bytes 5242880 | tf_op jit(solution)/shard_map/pallas_call | solution.py:97
  7.4 0.0 copy-start
  7.4 0.9 %reshape.84 = f32[2,4,4,8,32]{4,3,2,1,0:T(8,128)S(1)} reshape(f32[2,16,256]{2,1,0:T(8,128)} %get-tuple-element.8) | data formatting | bytes 65536 | tf_op jit(solution)/shard_map/reshape | solution.py:140
  8.4 0.1 reduce-precision_convert_fusion.1
  8.4 0.2 pad_maximum_fusion.1
  8.6 0.1 convert_element_type.21
  8.8 0.0 copy-done
  8.8 0.1 pad_maximum_fusion
  8.9 36.3 %all_to_all.5 = bf16[32,134,128]{2,1,0:T(8,128)(2,1)S(1)} all-to-all(bf16[32,134,128]{2,1,0:T(8,128)(2,1)S(1)} %pad_maximum_fusion), channel_id=1, replica_groups=mesh['ctx'=4,'row'=8] {'row','ctx'}, dimensions={0} | all-to-all | bytes 2195456 | tf_op jit(solution)/shard_map/all_to_all | solution.py:149
  45.2 0.2 reshape.87
  45.6 0.1 sub.44
  45.7 0.1 squeeze.11
  45.8 0.7 %multiply_reduce_fusion = f32[8,128,128]{2,1,0:T(8,128)S(1)} fusion(bf16[8,4,134,128]{3,2,1,0:T(8,128)(2,1)S(1)} %bitcast.34, f32[8,4,128]{2,1,0:T(4,128)S(1)} %subtract_exponential_fusion), kind=kLoop, calls=%fused_computation | loop fusion | flops 1441792 | bytes 1589248 | tf_op jit(solution)/shard_map/reduce_sum | solution.py:162
  46.6 0.2 divide_convert_fusion
  46.8 0.1 copy.14
  46.9 0.7 %copy.19 = bf16[32,8,4,128]{3,1,2,0:T(8,128)(2,1)} copy(bf16[32,8,4,128]{3,2,1,0:T(4,128)(2,1)S(1)} %bitcast.37) | data formatting | bytes 524288
  (8 shorter events, 0.2 us)
Async XLA Ops:
  7.4 1.4 %copy-start = (bf16[8,16,32,128]{3,2,1,0:T(8,128)(2,1)S(1)}, bf16[8,16,32,128]{3,2,1,0:T(8,128)(2,1)}, u32[]{:S(2)}) copy-start(bf16[8,16,32,128]{3,2,1,0:T(8,128)(2,1)} %get-tuple-element.7) | copy-start | bytes 3145732

commit v19 on v17

--- a/solution.py
+++ b/solution.py
@@ -161,8 +161,9 @@
     total_sum = jnp.sum(totals * weight, axis=1)
     numerator = jnp.sum(part_in.astype(jnp.float32) * weight[..., None], axis=1)
     attended = numerator / total_sum[..., None]
-    attended_low = jnp.transpose(attended, (0, 2, 1, 3)).reshape(row_count, share_width)
-    return attended_low.astype(jnp.bfloat16)
+    attended_low = jnp.transpose(attended, (0, 2, 1, 3)).astype(jnp.bfloat16)
+    attended_low = with_layout_constraint(attended_low, Layout(major_to_minor=(0, 1, 2, 3)))
+    return attended_low.reshape(row_count, share_width)
 
 
 def solution(mesh):

time: 47.8 us -> 48.1 us (level)
  no operation moved by 1% of the time
where the time goes in v19:
time: 48.1 us; the launch traced here: 47.9 us
  blocking collectives  36.3 us (75%)
  Pallas kernels  7.37 us (15%)
  local copies, waits for them, and re-layouts  2.44 us (5%)
  other arithmetic  1.67 us (3%)
    all_to_all x1, blocking collectives, local(): arrived = lax.all_to_all(payload, ('row', 'ctx'), 0, 0, tiled=True)  36.3 us
    pallas_call x1, Pallas kernels, local_attention(): pl.pallas_call(functools.partial(attention_kernel, shape), grid_spec=grid...  7.37 us

profile of v19, /device:TPU:0, one launch (start us, length us, event | category | flops | bytes accessed | tf_op | source)
XLA Modules:
  0.0 47.9 jit_solution(1744746210114460695)
XLA Ops:
  0.0 7.4 %shard_map.55 = (bf16[8,16,32,128]{3,2,1,0:T(8,128)(2,1)}, f32[2,16,256]{2,1,0:T(8,128)}) custom-call(s32[2,8]{1,0:T(2,128)} %list_ref.1, s32[2]{0:T(128)} %count_ref.1, s32[1]{0:T(128)} %bitcast.first_ref, bf16[256,2048]{1,0:T(8,128)(2,1)} %q_ref.1, bf16[384,2048]{1,0:T(8,128)(2,1)} %k_ref.1, bf16[384,2048]{1,0:T(8,128)(2,1)} %v_ref.1), custom_call_target="tpu_custom_call" | custom-call | flops 805306368 | bytes 5242880 | tf_op jit(solution)/shard_map/pallas_call | solution.py:97
  7.4 0.0 copy-start
  7.4 0.9 %reshape.85 = f32[2,4,4,8,32]{4,3,2,1,0:T(8,128)S(1)} reshape(f32[2,16,256]{2,1,0:T(8,128)} %get-tuple-element.8) | data formatting | bytes 65536 | tf_op jit(solution)/shard_map/reshape | solution.py:140
  8.4 0.1 reduce-precision_convert_fusion.1
  8.4 0.2 pad_maximum_fusion.1
  8.6 0.1 convert_element_type.18
  8.8 0.0 copy-done
  8.8 0.1 pad_maximum_fusion
  8.9 36.3 %all_to_all.5 = bf16[32,134,128]{2,1,0:T(8,128)(2,1)S(1)} all-to-all(bf16[32,134,128]{2,1,0:T(8,128)(2,1)S(1)} %pad_maximum_fusion), channel_id=1, replica_groups=mesh['ctx'=4,'row'=8] {'row','ctx'}, dimensions={0} | all-to-all | bytes 2195456 | tf_op jit(solution)/shard_map/all_to_all | solution.py:149
  45.2 0.2 reshape.89
  45.6 0.1 sub.44
  45.7 0.1 squeeze.11
  45.8 0.7 %multiply_reduce_fusion = f32[8,128,128]{2,1,0:T(8,128)S(1)} fusion(bf16[8,4,134,128]{3,2,1,0:T(8,128)(2,1)S(1)} %bitcast.36, f32[8,4,128]{2,1,0:T(4,128)S(1)} %subtract_exponential_fusion), kind=kLoop, calls=%fused_computation | loop fusion | flops 1441792 | bytes 1589248 | tf_op jit(solution)/shard_map/reduce_sum | solution.py:162
  46.6 0.1 copy.16
  46.7 0.4 fusion
  47.1 0.7 %copy.24 = bf16[32,8,4,128]{3,1,2,0:T(8,128)(2,1)} copy(bf16[32,8,4,128]{3,2,1,0:T(4,128)(2,1)S(1)} %bitcast.38) | data formatting | bytes 524288
  (8 shorter events, 0.2 us)
Async XLA Ops:
  7.4 1.4 %copy-start = (bf16[8,16,32,128]{3,2,1,0:T(8,128)(2,1)S(1)}, bf16[8,16,32,128]{3,2,1,0:T(8,128)(2,1)}, u32[]{:S(2)}) copy-start(bf16[8,16,32,128]{3,2,1,0:T(8,128)(2,1)} %get-tuple-element.7) | copy-start | bytes 3145732

commit v20 on v17

--- a/solution.py
+++ b/solution.py
@@ -139,6 +139,7 @@
     part_low = part.reshape(owners * shards, head_share * per_owner, HEAD_DIM)
     stats = jnp.transpose(stat.reshape(2, shards, head_share, owners, per_owner), (3, 1, 0, 2, 4))
     stats = stats.reshape(owners * shards, 2, head_share, per_owner)
+    stats = with_layout_constraint(stats, Layout(major_to_minor=(0, 1, 2, 3)))
     stat_count = 3 * 2 * head_share * per_owner
     stat_rows = -(-stat_count // HEAD_DIM)
     stat_low = split_three(stats).reshape(owners * shards, stat_count)

time: 47.8 us -> 47.9 us (level)
    reshape x1 -> x2, local copies, waits for them, and re-layouts: 0.93 us -> 0.97 us  [local(): stat.reshape(2, shards, head_share, owners, per_owner)]
where the time goes in v20:
time: 47.9 us; the launch traced here: 47.7 us
  blocking collectives  36.3 us (76%)
  Pallas kernels  7.37 us (15%)
  local copies, waits for them, and re-layouts  2.5 us (5%)
  other arithmetic  1.44 us (3%)
    all_to_all x1, blocking collectives, local(): arrived = lax.all_to_all(payload, ('row', 'ctx'), 0, 0, tiled=True)  36.3 us
    pallas_call x1, Pallas kernels, local_attention(): pl.pallas_call(functools.partial(attention_kernel, shape), grid_spec=grid...  7.37 us
    reshape x2, local copies, waits for them, and re-layouts, local(): stat.reshape(2, shards, head_share, owners, per_owner)  0.97 us

profile of v20, /device:TPU:0, one launch (start us, length us, event | category | flops | bytes accessed | tf_op | source)
XLA Modules:
  0.0 47.7 jit_solution(16890148706952783240)
XLA Ops:
  0.0 7.4 %shard_map.55 = (bf16[8,16,32,128]{3,2,1,0:T(8,128)(2,1)}, f32[2,16,256]{2,1,0:T(8,128)}) custom-call(s32[2,8]{1,0:T(2,128)} %list_ref.1, s32[2]{0:T(128)} %count_ref.1, s32[1]{0:T(128)} %bitcast.first_ref, bf16[256,2048]{1,0:T(8,128)(2,1)} %q_ref.1, bf16[384,2048]{1,0:T(8,128)(2,1)} %k_ref.1, bf16[384,2048]{1,0:T(8,128)(2,1)} %v_ref.1), custom_call_target="tpu_custom_call" | custom-call | flops 805306368 | bytes 5242880 | tf_op jit(solution)/shard_map/pallas_call | solution.py:97
  7.4 0.0 copy-start
  7.4 0.9 %reshape.45 = f32[2,4,4,8,32]{4,3,2,1,0:T(8,128)S(1)} reshape(f32[2,16,256]{2,1,0:T(8,128)} %get-tuple-element.8) | data formatting | bytes 65536 | tf_op jit(solution)/shard_map/reshape | solution.py:140
  8.4 0.1 reduce-precision_convert_fusion.1
  8.4 0.2 pad_maximum_fusion.1
  8.6 0.1 copy.18
  8.7 0.1 reshape.49
  8.9 0.0 copy-done
  8.9 0.1 pad_maximum_fusion
  9.0 36.3 %all_to_all.5 = bf16[32,134,128]{2,1,0:T(8,128)(2,1)S(1)} all-to-all(bf16[32,134,128]{2,1,0:T(8,128)(2,1)S(1)} %pad_maximum_fusion), channel_id=1, replica_groups=mesh['ctx'=4,'row'=8] {'row','ctx'}, dimensions={0} | all-to-all | bytes 2195456 | tf_op jit(solution)/shard_map/all_to_all | solution.py:150
  45.3 0.2 reshape.48
  45.7 0.1 sub.26
  45.8 0.1 squeeze.11
  45.9 0.7 %multiply_reduce_fusion = f32[8,128,128]{2,1,0:T(8,128)S(1)} fusion(bf16[8,4,134,128]{3,2,1,0:T(8,128)(2,1)S(1)} %bitcast.42, f32[8,4,128]{2,1,0:T(4,128)S(1)} %subtract_exponential_fusion), kind=kLoop, calls=%fused_computation | loop fusion | flops 1441792 | bytes 1589248 | tf_op jit(solution)/shard_map/reduce_sum | solution.py:163
  46.6 0.2 divide_convert_fusion
  46.8 0.1 copy.17
  47.0 0.7 %copy.24 = bf16[32,8,4,128]{3,1,2,0:T(8,128)(2,1)} copy(bf16[32,8,4,128]{3,2,1,0:T(4,128)(2,1)S(1)} %bitcast.45) | data formatting | bytes 524288
  (7 shorter events, 0.2 us)
Async XLA Ops:
  7.4 1.5 %copy-start = (bf16[8,16,32,128]{3,2,1,0:T(8,128)(2,1)S(1)}, bf16[8,16,32,128]{3,2,1,0:T(8,128)(2,1)}, u32[]{:S(2)}) copy-start(bf16[8,16,32,128]{3,2,1,0:T(8,128)(2,1)} %get-tuple-element.7) | copy-start | bytes 3145732

commit v21 on v19

--- a/solution.py
+++ b/solution.py
@@ -139,6 +139,7 @@
     part_low = part.reshape(owners * shards, head_share * per_owner, HEAD_DIM)
     stats = jnp.transpose(stat.reshape(2, shards, head_share, owners, per_owner), (3, 1, 0, 2, 4))
     stats = stats.reshape(owners * shards, 2, head_share, per_owner)
+    stats = with_layout_constraint(stats, Layout(major_to_minor=(0, 1, 2, 3)))
     stat_count = 3 * 2 * head_share * per_owner
     stat_rows = -(-stat_count // HEAD_DIM)
     stat_low = split_three(stats).reshape(owners * shards, stat_count)

time: 48.1 us -> 48.1 us (level)
    reshape x1 -> x2, local copies, waits for them, and re-layouts: 0.93 us -> 0.97 us  [local(): stat.reshape(2, shards, head_share, owners, per_owner)]
where the time goes in v21:
time: 48.1 us; the launch traced here: 47.9 us
  blocking collectives  36.3 us (75%)
  Pallas kernels  7.37 us (15%)
  local copies, waits for them, and re-layouts  2.49 us (5%)
  other arithmetic  1.68 us (3%)
    all_to_all x1, blocking collectives, local(): arrived = lax.all_to_all(payload, ('row', 'ctx'), 0, 0, tiled=True)  36.3 us
    pallas_call x1, Pallas kernels, local_attention(): pl.pallas_call(functools.partial(attention_kernel, shape), grid_spec=grid...  7.37 us
    reshape x2, local copies, waits for them, and re-layouts, local(): stat.reshape(2, shards, head_share, owners, per_owner)  0.97 us

profile of v21, /device:TPU:0, one launch (start us, length us, event | category | flops | bytes accessed | tf_op | source)
XLA Modules:
  0.0 47.9 jit_solution(3607106006590258367)
XLA Ops:
  0.0 7.4 %shard_map.55 = (bf16[8,16,32,128]{3,2,1,0:T(8,128)(2,1)}, f32[2,16,256]{2,1,0:T(8,128)}) custom-call(s32[2,8]{1,0:T(2,128)} %list_ref.1, s32[2]{0:T(128)} %count_ref.1, s32[1]{0:T(128)} %bitcast.first_ref, bf16[256,2048]{1,0:T(8,128)(2,1)} %q_ref.1, bf16[384,2048]{1,0:T(8,128)(2,1)} %k_ref.1, bf16[384,2048]{1,0:T(8,128)(2,1)} %v_ref.1), custom_call_target="tpu_custom_call" | custom-call | flops 805306368 | bytes 5242880 | tf_op jit(solution)/shard_map/pallas_call | solution.py:97
  7.4 0.0 copy-start
  7.4 0.9 %reshape.46 = f32[2,4,4,8,32]{4,3,2,1,0:T(8,128)S(1)} reshape(f32[2,16,256]{2,1,0:T(8,128)} %get-tuple-element.8) | data formatting | bytes 65536 | tf_op jit(solution)/shard_map/reshape | solution.py:140
  8.4 0.1 reduce-precision_convert_fusion.1
  8.4 0.2 pad_maximum_fusion.1
  8.6 0.1 copy.20
  8.7 0.1 reshape.51
  8.9 0.0 copy-done
  8.9 0.1 pad_maximum_fusion
  9.0 36.3 %all_to_all.5 = bf16[32,134,128]{2,1,0:T(8,128)(2,1)S(1)} all-to-all(bf16[32,134,128]{2,1,0:T(8,128)(2,1)S(1)} %pad_maximum_fusion), channel_id=1, replica_groups=mesh['ctx'=4,'row'=8] {'row','ctx'}, dimensions={0} | all-to-all | bytes 2195456 | tf_op jit(solution)/shard_map/all_to_all | solution.py:150
  45.3 0.2 reshape.50
  45.7 0.1 sub.26
  45.8 0.1 squeeze.11
  45.9 0.7 %multiply_reduce_fusion = f32[8,128,128]{2,1,0:T(8,128)S(1)} fusion(bf16[8,4,134,128]{3,2,1,0:T(8,128)(2,1)S(1)} %bitcast.44, f32[8,4,128]{2,1,0:T(4,128)S(1)} %subtract_exponential_fusion), kind=kLoop, calls=%fused_computation | loop fusion | flops 1441792 | bytes 1589248 | tf_op jit(solution)/shard_map/reduce_sum | solution.py:163
  46.6 0.1 copy.19
  46.7 0.4 fusion
  47.2 0.7 %copy.29 = bf16[32,8,4,128]{3,1,2,0:T(8,128)(2,1)} copy(bf16[32,8,4,128]{3,2,1,0:T(4,128)(2,1)S(1)} %bitcast.46) | data formatting | bytes 524288
  (7 shorter events, 0.2 us)
Async XLA Ops:
  7.4 1.5 %copy-start = (bf16[8,16,32,128]{3,2,1,0:T(8,128)(2,1)S(1)}, bf16[8,16,32,128]{3,2,1,0:T(8,128)(2,1)}, u32[]{:S(2)}) copy-start(bf16[8,16,32,128]{3,2,1,0:T(8,128)(2,1)} %get-tuple-element.7) | copy-start | bytes 3145732
